TPU v7x, 128 devices: a whole 4x4x4 slice. The times are simulated.
128 devices in a mesh: group: 16 (over z, x), local: 8 (over y, core).
Axes of the slice: x: 4, y: 4, z: 4, core: 2. Of those that a mesh axis runs over, the one named last changes fastest.
Arguments:
- tokens: bfloat16 [2048, 3584], P(('group', 'local')), may hold values from -6 to 6
- expert_ids: int32 [2048, 8], P(('group', 'local')), may hold values from 0 to 127, as said below
- gate_codes: int32 [2048, 8], P(('group', 'local')), may hold values from 1 to 1024
- w_gate: bfloat16 [128, 3584, 1024], P(('group', 'local')), may hold values from -0.09375 to 0.09375
- w_up: bfloat16 [128, 3584, 1024], P(('group', 'local')), may hold values from -0.09375 to 0.09375
- w_down: bfloat16 [128, 1024, 3584], P(('group', 'local')), may hold values from -0.1875 to 0.1875
Outputs:
- mixed: bfloat16 [2048, 3584], P(('group', 'local'))
Inputs may be any that keep to these rules, and one draw needn't show every extreme that they name: `expert_ids`: each row names 8 different experts, and they lie within at most 4 node groups, node group g holding experts g * 8 to (g + 1) * 8 - 1.
All inputs are finite; a program needn't handle non-finite values.
Results may differ from a plain program's by a relative error of at most 0.0057.
Values may be sent and summed in bfloat16 or wider, within the bound.
No kernel may reach another device: no remote copies, remote signals or barrier semaphores. Data moves between devices by JAX's collectives and lax.ppermute only.
A program may use at most 128 MiB of HBM per device.

v0:
```python
import jax
import jax.numpy as jnp
from jax import lax
from jax.sharding import PartitionSpec as P


def expert_rows(rows, gate_mat, up_mat, down_mat):
    gate_part = jnp.dot(rows, gate_mat, preferred_element_type=jnp.float32)
    up_part = jnp.dot(rows, up_mat, preferred_element_type=jnp.float32)
    hidden = (jax.nn.silu(gate_part) * up_part).astype(jnp.bfloat16)
    return jnp.dot(hidden, down_mat, preferred_element_type=jnp.float32).astype(jnp.bfloat16)


def local(tokens, expert_ids, gate_codes, w_gate, w_up, w_down):
    tok_rows, width = tokens.shape
    top = expert_ids.shape[1]
    num_groups = lax.axis_size("group")
    num_local = lax.axis_size("local")
    experts = num_groups * num_local
    capacity = 2 * tok_rows * top // experts
    total_slots = experts * capacity
    expert_range = jnp.arange(experts, dtype=jnp.int32)
    onehot = (expert_ids[:, :, None] == expert_range[None, None, :]).astype(jnp.int32)
    present = jnp.sum(onehot, axis=1)
    before = jnp.cumsum(present, axis=0) - present
    slot_rank = jnp.sum(onehot * before[:, None, :], axis=2)
    kept = slot_rank < capacity
    slot_index = jnp.where(kept, expert_ids * capacity + slot_rank, total_slots)
    flat_index = slot_index.reshape(-1)
    token_index = jnp.broadcast_to(jnp.arange(tok_rows, dtype=jnp.int32)[:, None], expert_ids.shape)
    slot_token = (
        jnp.zeros((total_slots,), jnp.int32)
        .at[flat_index]
        .set(token_index.reshape(-1), mode="drop")
    )
    slot_live = jnp.zeros((total_slots,), jnp.bool_).at[flat_index].set(True, mode="drop")
    outgoing = jnp.where(slot_live[:, None], tokens[slot_token], jnp.zeros((), jnp.bfloat16))
    counts = jnp.minimum(jnp.sum(present, axis=0), capacity)
    got_rows, got_counts = (
        lax.all_to_all(
            outgoing.reshape(experts, capacity, width),
            ("group", "local"),
            split_axis=0,
            concat_axis=0,
            tiled=True,
        ),
        lax.all_to_all(
            counts.reshape(experts, 1), ("group", "local"), split_axis=0, concat_axis=0, tiled=True
        ),
    )
    rows_in = got_rows.reshape(total_slots, width)
    counts_in = got_counts.reshape(experts)
    slot_pos = jnp.arange(total_slots, dtype=jnp.int32) % capacity
    live_in = slot_pos < jnp.repeat(counts_in, capacity)
    gate_mat = w_gate[0]
    up_mat = w_up[0]
    down_mat = w_down[0]
    produced = expert_rows(rows_in, gate_mat, up_mat, down_mat)
    produced = jnp.where(live_in[:, None], produced, jnp.zeros((), jnp.bfloat16))
    returned = lax.all_to_all(
        produced.reshape(experts, capacity, width),
        ("group", "local"),
        split_axis=0,
        concat_axis=0,
        tiled=True,
    )
    back_flat = returned.reshape(total_slots, width)
    picked = back_flat[jnp.minimum(flat_index, total_slots - 1)].reshape(tok_rows, top, width)
    weight = jnp.where(kept, gate_codes.astype(jnp.float32) / 1024.0, jnp.zeros((), jnp.float32))
    mixed = jnp.sum(weight[:, :, None] * picked.astype(jnp.float32), axis=1)
    return mixed.astype(jnp.bfloat16)


def solution(mesh):
    placed = (
        P(("group", "local"), None),
        P(("group", "local"), None),
        P(("group", "local"), None),
        P(("group", "local"), None, None),
        P(("group", "local"), None, None),
        P(("group", "local"), None, None),
    )
    return jax.shard_map(
        local, mesh=mesh, in_specs=placed, out_specs=P(("group", "local"), None), check_vma=False
    )
```

profile of v0, /device:TPU:1, one launch (start us, length us, event | category | flops | bytes accessed | tf_op | source)
XLA Modules:
  0.0 123.4 jit_solution(10705972033500018765)
XLA Ops:
  0.0 0.8 copy.21
  0.8 0.1 convert_reduce_fusion.1
  0.9 0.4 select_reduce_fusion
  1.4 0.7 copy.23
  2.1 11.5 %all-to-all-start = ((s32[128,1,1]{2,1,0:T(1,128)}), s32[128,1,1]{2,1,0:T(1,128)S(1)}, u32[]{:S(2)}, u32[]{:S(2)}) async-start(s32[128,1,1]{2,1,0:T(1,128)} %copy.23), calls=%async_computation | async-start | bytes 131072 | tf_op jit(solution)/shard_map/all_to_all | solution.py:47
  13.8 1.0 scatter_custom_fusion.1
  14.8 1.7 %gather_fusion = bf16[256,3584]{1,0:T(8,128)(2,1)S(1)} fusion(bf16[16,3584]{1,0:T(8,128)(2,1)S(1)} %copy-done, s32[1024]{0:T(1024)S(1)} %pad_clamp_fusion.1), kind=kCustom, calls=%fused_computation | custom fusion | bytes 3671040 | tf_op jit(solution)/shard_map/gather | solution.py:37
  16.6 1.7 %gather.9 = bf16[128,2,3584]{2,1,0:T(2,128)(2,1)} reshape(bf16[256,3584]{1,0:T(8,128)(2,1)S(1)} %gather_fusion) | data formatting | bytes 3670016 | tf_op jit(solution)/shard_map/gather | solution.py:37
  18.3 1.0 scatter_custom_fusion
  19.3 0.2 broadcast_in_dim.63
  19.4 4.5 %broadcast_select_fusion = bf16[128,2,3584]{2,1,0:T(2,128)(2,1)} fusion(bf16[128,2,3584]{2,1,0:T(2,128)(2,1)} %gather.9, pred[128,2]{1,0:T(8,128)(4,1)S(1)} %broadcast_in_dim.63), kind=kLoop, calls=%fused_computation.12 | loop fusion | flops 917504 | bytes 3670272 | tf_op jit(solution)/shard_map/jit(_where)/select_n | solution.py:37
  23.9 9.8 %all-to-all-start.1 = ((bf16[128,2,3584]{2,1,0:T(2,128)(2,1)}), bf16[128,2,3584]{2,1,0:T(2,128)(2,1)S(1)}, u32[]{:S(2)}, u32[]{:S(2)}) async-start(bf16[128,2,3584]{2,1,0:T(2,128)(2,1)} %broadcast_select_fusion), calls=%async_computation.1 | async-start | bytes 3670016 | tf_op jit(solution)/shard_map/all_to_all | solution.py:40
  33.7 2.4 %reduce.1 = s32[128]{0:T(128)S(1)} reduce(s32[128,1,1]{2,1,0:T(1,128)S(1)} %all-to-all-done, s32[]{:T(128)} %constant.14.clone.1), dimensions={1,2}, to_apply=%all_to_all.10.reduce_sub_computation | reduce | bytes 1028 | tf_op jit(solution)/shard_map/all_to_all | solution.py:47
  36.1 0.2 reshape.119
  36.3 24.6 %all-to-all-done.1 = bf16[128,2,3584]{2,1,0:T(2,128)(2,1)S(1)} async-done(((bf16[128,2,3584]{2,1,0:T(2,128)(2,1)}), bf16[128,2,3584]{2,1,0:T(2,128)(2,1)S(1)}, u32[]{:S(2)}, u32[]{:S(2)}) %all-to-all-start.1) | async-done | bytes 1835040 | tf_op jit(solution)/shard_map/all_to_all | solution.py:40
  60.9 1.7 %reshape.122 = bf16[256,3584]{1,0:T(8,128)(2,1)} reshape(bf16[128,2,3584]{2,1,0:T(2,128)(2,1)S(1)} %all-to-all-done.1) | data formatting | bytes 3670016 | tf_op jit(solution)/shard_map/reshape | solution.py:51
  62.6 5.8 %fusion.4 = f32[256,1024]{1,0:T(8,128)S(1)} fusion(bf16[256,3584]{1,0:T(8,128)(2,1)} %reshape.122, bf16[1,3584,1024]{2,1,0:T(8,128)(2,1)} %param.9), kind=kOutput, calls=%fused_computation.8 | convolution fusion | flops 1879048192 | bytes 10223616 | tf_op jit(solution)/shard_map/dot_general | solution.py:8
  68.4 10.6 %fusion.9 = bf16[256,3584]{1,0:T(8,128)(2,1)} fusion(bf16[1,1024,3584]{2,1,0:T(8,128)(2,1)} %param.11, pred[256]{0:T(512)(128)(4,1)S(1)} %fusion.22, bf16[256,3584]{1,0:T(8,128)(2,1)S(1)} %copy-done.1, bf16[1,3584,1024]{2,1,0:T(8,128)(2,1)} %param.10, f32[256,1024]{1,0:T(8,128)S(1)} %fusion.4), kind=kOutput, calls=%fused_computation.11 | convolution fusion | flops 3761504256 | bytes 19398912 | tf_op jit(solution)/shard_map/dot_general | solution.py:11
  79.0 4.8 %reshape.123 = bf16[128,2,3584]{2,1,0:T(2,128)(2,1)} reshape(bf16[256,3584]{1,0:T(8,128)(2,1)} %fusion.9) | data formatting | bytes 3670016 | tf_op jit(solution)/shard_map/reshape | solution.py:61
  83.8 5.9 %all-to-all-start.2 = ((bf16[128,2,3584]{2,1,0:T(2,128)(2,1)}), bf16[128,2,3584]{2,1,0:T(2,128)(2,1)}, u32[]{:S(2)}, u32[]{:S(2)}) async-start(bf16[128,2,3584]{2,1,0:T(2,128)(2,1)} %reshape.123), calls=%async_computation.2 | async-start | bytes 3670016 | tf_op jit(solution)/shard_map/all_to_all | solution.py:60
  89.9 27.0 %all-to-all-done.2 = bf16[128,2,3584]{2,1,0:T(2,128)(2,1)} async-done(((bf16[128,2,3584]{2,1,0:T(2,128)(2,1)}), bf16[128,2,3584]{2,1,0:T(2,128)(2,1)}, u32[]{:S(2)}, u32[]{:S(2)}) %all-to-all-start.2) | async-done | bytes 1835040 | tf_op jit(solution)/shard_map/all_to_all | solution.py:60
  116.9 4.1 %reshape.124 = bf16[256,3584]{1,0:T(8,128)(2,1)S(1)} reshape(bf16[128,2,3584]{2,1,0:T(2,128)(2,1)} %all-to-all-done.2) | data formatting | bytes 3670016 | tf_op jit(solution)/shard_map/reshape | solution.py:67
  120.9 1.1 gather_fusion.1
  122.0 1.3 %fusion.12 = bf16[16,3584]{1,0:T(8,128)(2,1)} fusion(bf16[128,3584]{1,0:T(8,128)(2,1)S(1)} %gather_fusion.1, f32[16,8]{1,0:T(8,128)S(1)} %multiply_select_fusion), kind=kLoop, calls=%fused_computation.14 | loop fusion | flops 1318912 | bytes 1032704 | tf_op jit(solution)/shard_map/reduce_sum | solution.py:70
  (23 shorter events, 0.4 us)
Async XLA Ops:
  0.0 14.8 %copy-start = (bf16[16,3584]{1,0:T(8,128)(2,1)S(1)}, bf16[16,3584]{1,0:T(8,128)(2,1)}, u32[]{:S(2)}) copy-start(bf16[16,3584]{1,0:T(8,128)(2,1)} %param.6) | copy-start | bytes 344068
  2.1 21.8 %all-to-all-start = ((s32[128,1,1]{2,1,0:T(1,128)}), s32[128,1,1]{2,1,0:T(1,128)S(1)}, u32[]{:S(2)}, u32[]{:S(2)}) async-start(s32[128,1,1]{2,1,0:T(1,128)} %copy.23), calls=%async_computation | async-start | bytes 131072 | tf_op jit(solution)/shard_map/all_to_all | solution.py:47
  23.9 37.0 %all-to-all-start.1 = ((bf16[128,2,3584]{2,1,0:T(2,128)(2,1)}), bf16[128,2,3584]{2,1,0:T(2,128)(2,1)S(1)}, u32[]{:S(2)}, u32[]{:S(2)}) async-start(bf16[128,2,3584]{2,1,0:T(2,128)(2,1)} %broadcast_select_fusion), calls=%async_computation.1 | async-start | bytes 3670016 | tf_op jit(solution)/shard_map/all_to_all | solution.py:40
  62.6 5.8 %copy-start.1 = (bf16[256,3584]{1,0:T(8,128)(2,1)S(1)}, bf16[256,3584]{1,0:T(8,128)(2,1)}, u32[]{:S(2)}) copy-start(bf16[256,3584]{1,0:T(8,128)(2,1)} %reshape.122) | copy-start | bytes 5505028
  83.8 5.9 %copy-start.2 = (s32[16,8]{0,1:T(8,128)S(1)}, s32[16,8]{0,1:T(8,128)}, u32[]{:S(2)}) copy-start(s32[16,8]{0,1:T(8,128)} %param.8) | copy-start | bytes 1540
  83.8 33.0 %all-to-all-start.2 = ((bf16[128,2,3584]{2,1,0:T(2,128)(2,1)}), bf16[128,2,3584]{2,1,0:T(2,128)(2,1)}, u32[]{:S(2)}, u32[]{:S(2)}) async-start(bf16[128,2,3584]{2,1,0:T(2,128)(2,1)} %reshape.123), calls=%async_computation.2 | async-start | bytes 3670016 | tf_op jit(solution)/shard_map/all_to_all | solution.py:60
where the time goes:
time: 124 us; the launch traced here: 123 us
  waiting for transfers between devices  51.6 us (42%)
  starting transfers between devices  27.2 us (22%)
  local copies, waits for them, and re-layouts  19.2 us (15%)
  matrix products  16.4 us (13%)
  other arithmetic  8.79 us (7%)
    all_to_all x1, waiting for transfers between devices, local(): lax.all_to_all(produced.reshape(experts, capacity, width), ('group', 'loc...  27 us
    all_to_all x1, waiting for transfers between devices, local(): lax.all_to_all(outgoing.reshape(experts, capacity, width), ('group', 'loc...  24.6 us
    all_to_all x1, starting transfers between devices, local(): lax.all_to_all(counts.reshape(experts, 1), ('group', 'local'), split_axis...  11.5 us
    dot_general x1, matrix products, expert_rows(): jnp.dot(hidden, down_mat, preferred_element_type=jnp.float32)  10.6 us
    all_to_all x1, starting transfers between devices, local(): lax.all_to_all(outgoing.reshape(experts, capacity, width), ('group', 'loc...  9.77 us
    all_to_all x1, starting transfers between devices, local(): lax.all_to_all(produced.reshape(experts, capacity, width), ('group', 'loc...  5.94 us
    dot_general x1, matrix products, expert_rows(): gate_part = jnp.dot(rows, gate_mat, preferred_element_type=jnp.float32)  5.82 us
    reshape x1, local copies, waits for them, and re-layouts, local(): produced.reshape(experts, capacity, width)  4.79 us
  transfers between devices with their start and end apart: 3, of which 2 were waited for; matrix products, arithmetic and copies ran while one was open for 10% of the time, Pallas kernels for 0%

commit v1 on v0

v1 whole, which is shorter than its diff:
```python
import jax
import jax.numpy as jnp
from jax import lax
from jax.sharding import PartitionSpec as P


def expert_rows(rows, gate_mat, up_mat, down_mat):
    gate_part = jnp.dot(rows, gate_mat, preferred_element_type=jnp.float32)
    up_part = jnp.dot(rows, up_mat, preferred_element_type=jnp.float32)
    hidden = (jax.nn.silu(gate_part) * up_part).astype(jnp.bfloat16)
    return jnp.dot(hidden, down_mat, preferred_element_type=jnp.float32).astype(jnp.bfloat16)


def local(tokens, expert_ids, gate_codes, w_gate, w_up, w_down):
    tok_rows, width = tokens.shape
    top = expert_ids.shape[1]
    num_groups = lax.axis_size("group")
    num_local = lax.axis_size("local")
    experts = num_groups * num_local
    capacity = 2 * tok_rows * top // experts
    total_slots = experts * capacity
    expert_range = jnp.arange(experts, dtype=jnp.int32)
    onehot = (expert_ids[:, :, None] == expert_range[None, None, :]).astype(jnp.int32)
    present = jnp.sum(onehot, axis=1)
    before = jnp.cumsum(present, axis=0) - present
    slot_rank = jnp.sum(onehot * before[:, None, :], axis=2)
    kept = slot_rank < capacity
    slot_index = jnp.where(kept, slot_rank * experts + expert_ids, total_slots)
    slot_range = jnp.arange(total_slots, dtype=jnp.int32)
    route_hit = slot_index[:, :, None] == slot_range[None, None, :]
    pick = jnp.any(route_hit, axis=1)
    outgoing = jnp.dot(
        pick.T.astype(jnp.bfloat16), tokens, preferred_element_type=jnp.float32
    ).astype(jnp.bfloat16)
    got_rows = lax.all_to_all(
        outgoing.reshape(capacity, experts, width),
        ("group", "local"),
        split_axis=1,
        concat_axis=1,
        tiled=True,
    )
    rows_in = got_rows.reshape(total_slots, width)
    produced = expert_rows(rows_in, w_gate[0], w_up[0], w_down[0])
    returned = lax.all_to_all(
        produced.reshape(capacity, experts, width),
        ("group", "local"),
        split_axis=1,
        concat_axis=1,
        tiled=True,
    )
    back_flat = returned.reshape(total_slots, width)
    weight = jnp.where(kept, gate_codes.astype(jnp.float32) / 1024.0, jnp.zeros((), jnp.float32))
    combine = jnp.sum(jnp.where(route_hit, weight[:, :, None], 0.0), axis=1)
    combine_hi = combine.astype(jnp.bfloat16)
    combine_lo = (combine - combine_hi.astype(jnp.float32)).astype(jnp.bfloat16)
    mixed = jnp.dot(combine_hi, back_flat, preferred_element_type=jnp.float32) + jnp.dot(
        combine_lo, back_flat, preferred_element_type=jnp.float32
    )
    return mixed.astype(jnp.bfloat16)


def solution(mesh):
    placed = (
        P(("group", "local"), None),
        P(("group", "local"), None),
        P(("group", "local"), None),
        P(("group", "local"), None, None),
        P(("group", "local"), None, None),
        P(("group", "local"), None, None),
    )
    return jax.shard_map(
        local, mesh=mesh, in_specs=placed, out_specs=P(("group", "local"), None), check_vma=False
    )
```

time: 124 us -> 94.1 us (0.76)
  blocking collectives: 0 us -> 38.5 us
  waiting for transfers between devices: 51.6 us -> 27.1 us
  starting transfers between devices: 27.2 us -> 4.94 us
  local copies, waits for them, and re-layouts: 19.2 us -> 7.74 us
  other arithmetic: 8.79 us -> 0.8 us
  matrix products: 16.4 us -> 14.5 us
    all_to_all x0 -> x1, blocking collectives: none -> 38.5 us  [local(): lax.all_to_all(outgoing.reshape(capacity, experts, width), ('group', 'loc...]
    all_to_all x3 -> x1, waiting for transfers between devices: 51.6 us -> 27.1 us  [local(): lax.all_to_all(produced.reshape(capacity, experts, width), ('group', 'loc...]
    all_to_all x3 -> x1, starting transfers between devices: 27.2 us -> 4.94 us  [local(): lax.all_to_all(produced.reshape(capacity, experts, width), ('group', 'loc...]
    select_n x4 -> x1, other arithmetic: 4.53 us -> 0.01 us  [local(): slot_index = jnp.where(kept, slot_rank * experts + expert_ids, total_slots)]
    gather x3 -> x0, local copies, waits for them, and re-layouts: 4.52 us -> none  [the longest x2 3.41 us: local(): tokens[slot_token]]
    reshape x6 -> x2, local copies, waits for them, and re-layouts: 10.8 us -> 6.5 us  [the longest x1 4.61 us: local(): produced.reshape(capacity, experts, width)]
    dot_general x1, matrix products: 5.82 us -> 2.05 us  [expert_rows(): gate_part = jnp.dot(rows, gate_mat, preferred_element_type=jnp.float32)]
    all_to_all x1 -> x0, other arithmetic: 2.35 us -> none  [local(): lax.all_to_all(counts.reshape(experts, 1), ('group', 'local'), split_axis...]
  transfers between devices with their start and end apart: 3 -> 1, of which waited for: 2 -> 1; matrix products, arithmetic and copies ran while one was open for 10% -> 0% of each run, Pallas kernels for 0% -> 0%
where the time goes in v1:
time: 94.1 us; the launch traced here: 93.8 us
  blocking collectives  38.5 us (41%)
  waiting for transfers between devices  27.1 us (29%)
  matrix products  14.5 us (15%)
  local copies, waits for them, and re-layouts  7.74 us (8%)
  starting transfers between devices  4.94 us (5%)
    all_to_all x1, blocking collectives, local(): lax.all_to_all(outgoing.reshape(capacity, experts, width), ('group', 'loc...  38.5 us
    all_to_all x1, waiting for transfers between devices, local(): lax.all_to_all(produced.reshape(capacity, experts, width), ('group', 'loc...  27.1 us
    dot_general x1, matrix products, expert_rows(): jnp.dot(hidden, down_mat, preferred_element_type=jnp.float32)  10.5 us
    all_to_all x1, starting transfers between devices, local(): lax.all_to_all(produced.reshape(capacity, experts, width), ('group', 'loc...  4.94 us
    reshape x1, local copies, waits for them, and re-layouts, local(): produced.reshape(capacity, experts, width)  4.61 us
    dot_general x1, matrix products, expert_rows(): gate_part = jnp.dot(rows, gate_mat, preferred_element_type=jnp.float32)  2.05 us
    reshape x1, local copies, waits for them, and re-layouts, local(): outgoing.reshape(capacity, experts, width)  1.89 us
  transfers between devices with their start and end apart: 1, of which 1 were waited for; matrix products, arithmetic and copies ran while one was open for 0% of the time, Pallas kernels for 0%

profile of v1, /device:TPU:1, one launch (start us, length us, event | category | flops | bytes accessed | tf_op | source)
XLA Modules:
  0.0 93.8 jit_solution(2599175679657599539)
XLA Ops:
  0.0 0.0 copy-start
  0.0 0.8 copy.22
  0.8 0.1 convert_reduce_fusion
  0.9 0.4 select_reduce_fusion.1
  1.4 0.1 fusion.19
  1.5 0.0 copy-done
  1.5 0.7 convolution_convert_fusion
  2.2 1.9 %copy.25 = bf16[2,128,3584]{2,0,1:T(2,128)(2,1)S(1)} copy(bf16[2,128,3584]{2,1,0:T(8,128)(2,1)S(1)} %bitcast.29) | data formatting | bytes 3670016 | tf_op jit(solution)/shard_map/reshape | solution.py:36
  4.1 0.0 copy-start.2
  4.1 38.5 %all_to_all.10 = bf16[2,128,3584]{2,0,1:T(2,128)(2,1)S(1)} all-to-all(bf16[2,128,3584]{2,0,1:T(2,128)(2,1)S(1)} %copy.25), channel_id=1, replica_groups=mesh['group'=16,'local'=8] {'group','local'}, dimensions={1} | all-to-all | bytes 3670016 | tf_op jit(solution)/shard_map/all_to_all | solution.py:35
  42.6 0.2 copy.26
  42.8 0.0 copy-done.2
  42.8 2.1 %fusion.4 = f32[256,1024]{1,0:T(8,128)S(1)} fusion(bf16[256,3584]{1,0:T(8,128)(2,1)S(1)} %bitcast.30, bf16[1,3584,1024]{2,1,0:T(8,128)(2,1)S(1)} %copy-done.2), kind=kOutput, calls=%fused_computation.4 | convolution fusion | flops 1879048192 | bytes 10223616 | tf_op jit(solution)/shard_map/dot_general | solution.py:8
  44.9 10.5 %fusion.6 = bf16[256,3584]{1,0:T(8,128)(2,1)} fusion(bf16[1,1024,3584]{2,1,0:T(8,128)(2,1)} %param.11, bf16[256,3584]{1,0:T(8,128)(2,1)S(1)} %bitcast.31, bf16[1,3584,1024]{2,1,0:T(8,128)(2,1)} %param.10, f32[256,1024]{1,0:T(8,128)S(1)} %fusion.4), kind=kOutput, calls=%fused_computation.6 | convolution fusion | flops 3760586752 | bytes 19398656 | tf_op jit(solution)/shard_map/dot_general | solution.py:11
  55.3 4.6 %copy.27 = bf16[2,128,3584]{2,0,1:T(2,128)(2,1)} copy(bf16[2,128,3584]{2,1,0:T(8,128)(2,1)} %bitcast.32) | data formatting | bytes 3670016 | tf_op jit(solution)/shard_map/reshape | solution.py:45
  59.9 0.0 copy-start.1
  59.9 4.9 %all-to-all-start.1 = ((bf16[2,128,3584]{2,0,1:T(2,128)(2,1)}), bf16[2,128,3584]{2,0,1:T(2,128)(2,1)S(1)}, u32[]{:S(2)}, u32[]{:S(2)}) async-start(bf16[2,128,3584]{2,0,1:T(2,128)(2,1)} %copy.27), calls=%async_computation.1 | async-start | bytes 3670016 | tf_op jit(solution)/shard_map/all_to_all | solution.py:44
  64.9 0.0 copy-done.1
  64.9 0.1 copy.24
  65.0 0.1 select_reduce_fusion
  65.1 27.1 %all-to-all-done.1 = bf16[2,128,3584]{2,0,1:T(2,128)(2,1)S(1)} async-done(((bf16[2,128,3584]{2,0,1:T(2,128)(2,1)}), bf16[2,128,3584]{2,0,1:T(2,128)(2,1)S(1)}, u32[]{:S(2)}, u32[]{:S(2)}) %all-to-all-start.1) | async-done | bytes 1835040 | tf_op jit(solution)/shard_map/all_to_all | solution.py:44
  92.2 0.2 copy.28
  92.4 0.3 fusion.21
  92.8 1.0 %fusion.9 = bf16[16,3584]{1,0:T(8,128)(2,1)} fusion(f32[16,3584]{1,0:T(8,128)S(1)} %fusion.21, bf16[256,3584]{1,0:T(8,128)(2,1)S(1)} %bitcast.28, f32[16,256]{1,0:T(8,128)S(1)} %select_reduce_fusion), kind=kOutput, calls=%fused_computation.9 | convolution fusion | flops 29491200 | bytes 2195456 | tf_op jit(solution)/shard_map/dot_general | solution.py:56
  (4 shorter events, 0.1 us)
Async XLA Ops:
  0.0 1.5 %copy-start = (bf16[16,3584]{1,0:T(8,128)(2,1)S(1)}, bf16[16,3584]{1,0:T(8,128)(2,1)}, u32[]{:S(2)}) copy-start(bf16[16,3584]{1,0:T(8,128)(2,1)} %param.6) | copy-start | bytes 344068
  4.1 38.7 %copy-start.2 = (bf16[1,3584,1024]{2,1,0:T(8,128)(2,1)S(1)}, bf16[1,3584,1024]{2,1,0:T(8,128)(2,1)}, u32[]{:S(2)}) copy-start(bf16[1,3584,1024]{2,1,0:T(8,128)(2,1)} %param.9) | copy-start | bytes 22020100
  59.9 4.9 %copy-start.1 = (s32[16,8]{0,1:T(8,128)S(1)}, s32[16,8]{0,1:T(8,128)}, u32[]{:S(2)}) copy-start(s32[16,8]{0,1:T(8,128)} %param.8) | copy-start | bytes 1540
  59.9 32.3 %all-to-all-start.1 = ((bf16[2,128,3584]{2,0,1:T(2,128)(2,1)}), bf16[2,128,3584]{2,0,1:T(2,128)(2,1)S(1)}, u32[]{:S(2)}, u32[]{:S(2)}) async-start(bf16[2,128,3584]{2,0,1:T(2,128)(2,1)} %copy.27), calls=%async_computation.1 | async-start | bytes 3670016 | tf_op jit(solution)/shard_map/all_to_all | solution.py:44

commit v2 on v1

--- a/solution.py
+++ b/solution.py
@@ -1,14 +1,60 @@
 import jax
 import jax.numpy as jnp
 from jax import lax
+from jax.experimental import pallas as pl
+from jax.experimental.pallas import tpu as pltpu
 from jax.sharding import PartitionSpec as P
 
+H_BLOCK = 256
 
-def expert_rows(rows, gate_mat, up_mat, down_mat):
-    gate_part = jnp.dot(rows, gate_mat, preferred_element_type=jnp.float32)
-    up_part = jnp.dot(rows, up_mat, preferred_element_type=jnp.float32)
-    hidden = (jax.nn.silu(gate_part) * up_part).astype(jnp.bfloat16)
-    return jnp.dot(hidden, down_mat, preferred_element_type=jnp.float32).astype(jnp.bfloat16)
+
+def mlp_kernel(x_ref, wg_ref, wu_ref, wd_ref, o_ref, acc_ref):
+    j = pl.program_id(0)
+    x = x_ref[...]
+    gate_part = jnp.dot(x, wg_ref[...], preferred_element_type=jnp.float32)
+    up_part = jnp.dot(x, wu_ref[...], preferred_element_type=jnp.float32)
+    hidden = (gate_part / (1.0 + jnp.exp(-gate_part)) * up_part).astype(jnp.bfloat16)
+    part = jnp.dot(hidden, wd_ref[...], preferred_element_type=jnp.float32)
+
+    @pl.when(j == 0)
+    def _():
+        acc_ref[...] = part
+
+    @pl.when(j > 0)
+    def _():
+        acc_ref[...] += part
+
+    @pl.when(j == pl.num_programs(0) - 1)
+    def _():
+        o_ref[...] = acc_ref[...].astype(o_ref.dtype)
+
+
+def expert_rows(rows, w_gate, w_up, w_down):
+    slots, width = rows.shape
+    hid = w_gate.shape[2]
+    steps = hid // H_BLOCK
+    cost = pl.CostEstimate(
+        flops=6 * slots * width * hid,
+        transcendentals=slots * hid,
+        bytes_accessed=2 * (3 * width * hid + 2 * slots * width),
+    )
+    return pl.pallas_call(
+        mlp_kernel,
+        grid=(steps,),
+        in_specs=[
+            pl.BlockSpec((slots, width), lambda j: (0, 0)),
+            pl.BlockSpec((None, width, H_BLOCK), lambda j: (0, 0, j)),
+            pl.BlockSpec((None, width, H_BLOCK), lambda j: (0, 0, j)),
+            pl.BlockSpec((None, H_BLOCK, width), lambda j: (0, j, 0)),
+        ],
+        out_specs=pl.BlockSpec((slots, width), lambda j: (0, 0)),
+        out_shape=jax.ShapeDtypeStruct((slots, width), jnp.bfloat16),
+        scratch_shapes=[pltpu.VMEM((slots, width), jnp.float32)],
+        compiler_params=pltpu.CompilerParams(
+            dimension_semantics=("arbitrary",), vmem_limit_bytes=48 * 1024 * 1024
+        ),
+        cost_estimate=cost,
+    )(rows, w_gate, w_up, w_down)
 
 
 def local(tokens, expert_ids, gate_codes, w_gate, w_up, w_down):
@@ -40,7 +86,7 @@
         tiled=True,
     )
     rows_in = got_rows.reshape(total_slots, width)
-    produced = expert_rows(rows_in, w_gate[0], w_up[0], w_down[0])
+    produced = expert_rows(rows_in, w_gate, w_up, w_down)
     returned = lax.all_to_all(
         produced.reshape(capacity, experts, width),
         ("group", "local"),
@@ -51,11 +97,11 @@
     back_flat = returned.reshape(total_slots, width)
     weight = jnp.where(kept, gate_codes.astype(jnp.float32) / 1024.0, jnp.zeros((), jnp.float32))
     combine = jnp.sum(jnp.where(route_hit, weight[:, :, None], 0.0), axis=1)
-    combine_hi = combine.astype(jnp.bfloat16)
-    combine_lo = (combine - combine_hi.astype(jnp.float32)).astype(jnp.bfloat16)
-    mixed = jnp.dot(combine_hi, back_flat, preferred_element_type=jnp.float32) + jnp.dot(
-        combine_lo, back_flat, preferred_element_type=jnp.float32
-    )
+    combine_hi = lax.reduce_precision(combine, exponent_bits=8, mantissa_bits=7)
+    combine_lo = combine - combine_hi
+    mixed = jnp.dot(
+        combine_hi.astype(jnp.bfloat16), back_flat, preferred_element_type=jnp.float32
+    ) + jnp.dot(combine_lo.astype(jnp.bfloat16), back_flat, preferred_element_type=jnp.float32)
     return mixed.astype(jnp.bfloat16)
 
 

time: 94.1 us -> 91.6 us (0.973)
  matrix products: 14.5 us -> 2.03 us
  Pallas kernels: 0 us -> 11.6 us
  local copies, waits for them, and re-layouts: 7.74 us -> 6.26 us
    dot_general x4 -> x2, matrix products: 13.9 us -> 1.36 us  [the longest x1 1.02 us: local(): jnp.dot(combine_lo.astype(jnp.bfloat16), back_flat, preferred_element_typ...]
    pallas_call x0 -> x1, Pallas kernels: none -> 11.6 us  [expert_rows(): pl.pallas_call(mlp_kernel, grid=(steps,), in_specs=[pl.BlockSpec((slots,...]
    reshape x1, local copies, waits for them, and re-layouts: 4.61 us -> 3.14 us  [local(): produced.reshape(capacity, experts, width)]
where the time goes in v2:
time: 91.6 us; the launch traced here: 91.3 us
  blocking collectives  38.5 us (42%)
  waiting for transfers between devices  27.1 us (30%)
  Pallas kernels  11.6 us (13%)
  local copies, waits for them, and re-layouts  6.26 us (7%)
  starting transfers between devices  4.9 us (5%)
  matrix products  2.03 us (2%)
    all_to_all x1, blocking collectives, local(): lax.all_to_all(outgoing.reshape(capacity, experts, width), ('group', 'loc...  38.5 us
    all_to_all x1, waiting for transfers between devices, local(): lax.all_to_all(produced.reshape(capacity, experts, width), ('group', 'loc...  27.1 us
    pallas_call x1, Pallas kernels, expert_rows(): pl.pallas_call(mlp_kernel, grid=(steps,), in_specs=[pl.BlockSpec((slots,...  11.6 us
    all_to_all x1, starting transfers between devices, local(): lax.all_to_all(produced.reshape(capacity, experts, width), ('group', 'loc...  4.9 us
    reshape x1, local copies, waits for them, and re-layouts, local(): produced.reshape(capacity, experts, width)  3.14 us
    reshape x1, local copies, waits for them, and re-layouts, local(): outgoing.reshape(capacity, experts, width)  1.89 us
  transfers between devices with their start and end apart: 1, of which 1 were waited for; matrix products, arithmetic and copies ran while one was open for 0% of the time, Pallas kernels for 0%

profile of v2, /device:TPU:1, one launch (start us, length us, event | category | flops | bytes accessed | tf_op | source)
XLA Modules:
  0.0 91.3 jit_solution(16374319508441504852)
XLA Ops:
  0.0 0.0 copy-start
  0.0 0.8 copy.23
  0.8 0.1 convert_reduce_fusion
  0.9 0.4 select_reduce_fusion.1
  1.4 0.1 fusion.1
  1.5 0.0 copy-done
  1.5 0.7 convolution_convert_fusion
  2.2 1.9 %copy.26 = bf16[2,128,3584]{2,0,1:T(2,128)(2,1)S(1)} copy(bf16[2,128,3584]{2,1,0:T(8,128)(2,1)S(1)} %bitcast.12) | data formatting | bytes 3670016 | tf_op jit(solution)/shard_map/reshape | solution.py:82
  4.1 38.5 %all_to_all.10 = bf16[2,128,3584]{2,0,1:T(2,128)(2,1)S(1)} all-to-all(bf16[2,128,3584]{2,0,1:T(2,128)(2,1)S(1)} %copy.26), channel_id=1, replica_groups=mesh['group'=16,'local'=8] {'group','local'}, dimensions={1} | all-to-all | bytes 3670016 | tf_op jit(solution)/shard_map/all_to_all | solution.py:81
  42.6 0.2 copy.27
  42.8 11.6 %shard_map.64 = bf16[256,3584]{1,0:T(8,128)(2,1)S(1)} custom-call(bf16[256,3584]{1,0:T(8,128)(2,1)S(1)} %bitcast.8, bf16[1,3584,1024]{2,1,0:T(8,128)(2,1)} %wg_ref.1, bf16[1,3584,1024]{2,1,0:T(8,128)(2,1)} %wu_ref.1, bf16[1,1024,3584]{2,1,0:T(8,128)(2,1)} %wd_ref.1), custom_call_target="tpu_custom_call" | custom-call | flops 5637144576 | bytes 25690112 | tf_op jit(solution)/shard_map/pallas_call | solution.py:41
  54.4 3.1 %copy.28 = bf16[2,128,3584]{2,0,1:T(2,128)(2,1)} copy(bf16[2,128,3584]{2,1,0:T(8,128)(2,1)S(1)} %bitcast.9) | data formatting | bytes 3670016 | tf_op jit(solution)/shard_map/reshape | solution.py:91
  57.5 0.0 copy-start.1
  57.5 4.9 %all-to-all-start.1 = ((bf16[2,128,3584]{2,0,1:T(2,128)(2,1)}), bf16[2,128,3584]{2,0,1:T(2,128)(2,1)S(1)}, u32[]{:S(2)}, u32[]{:S(2)}) async-start(bf16[2,128,3584]{2,0,1:T(2,128)(2,1)} %copy.28), calls=%async_computation.1 | async-start | bytes 3670016 | tf_op jit(solution)/shard_map/all_to_all | solution.py:90
  62.4 0.0 copy-done.1
  62.5 0.1 copy.25
  62.5 0.1 select_reduce_fusion
  62.7 27.1 %all-to-all-done.1 = bf16[2,128,3584]{2,0,1:T(2,128)(2,1)S(1)} async-done(((bf16[2,128,3584]{2,0,1:T(2,128)(2,1)}), bf16[2,128,3584]{2,0,1:T(2,128)(2,1)S(1)}, u32[]{:S(2)}, u32[]{:S(2)}) %all-to-all-start.1) | async-done | bytes 1835040 | tf_op jit(solution)/shard_map/all_to_all | solution.py:90
  89.8 0.2 copy.29
  90.0 0.3 fusion.4
  90.3 1.0 %fusion = bf16[16,3584]{1,0:T(8,128)(2,1)} fusion(f32[16,3584]{1,0:T(8,128)S(1)} %fusion.4, bf16[256,3584]{1,0:T(8,128)(2,1)S(1)} %bitcast.11, f32[16,256]{1,0:T(8,128)S(1)} %select_reduce_fusion), kind=kOutput, calls=%fused_computation.2 | convolution fusion | flops 29487104 | bytes 2195456 | tf_op jit(solution)/shard_map/dot_general | solution.py:104
  (4 shorter events, 0.1 us)
Async XLA Ops:
  0.0 1.5 %copy-start = (bf16[16,3584]{1,0:T(8,128)(2,1)S(1)}, bf16[16,3584]{1,0:T(8,128)(2,1)}, u32[]{:S(2)}) copy-start(bf16[16,3584]{1,0:T(8,128)(2,1)} %param.6) | copy-start | bytes 344068
  57.5 4.9 %copy-start.1 = (s32[16,8]{0,1:T(8,128)S(1)}, s32[16,8]{0,1:T(8,128)}, u32[]{:S(2)}) copy-start(s32[16,8]{0,1:T(8,128)} %param.8) | copy-start | bytes 1540
  57.5 32.3 %all-to-all-start.1 = ((bf16[2,128,3584]{2,0,1:T(2,128)(2,1)}), bf16[2,128,3584]{2,0,1:T(2,128)(2,1)S(1)}, u32[]{:S(2)}, u32[]{:S(2)}) async-start(bf16[2,128,3584]{2,0,1:T(2,128)(2,1)} %copy.28), calls=%async_computation.1 | async-start | bytes 3670016 | tf_op jit(solution)/shard_map/all_to_all | solution.py:90

commit v3 on v2

--- a/solution.py
+++ b/solution.py
@@ -8,51 +8,61 @@
 H_BLOCK = 256
 
 
-def mlp_kernel(x_ref, wg_ref, wu_ref, wd_ref, o_ref, acc_ref):
-    j = pl.program_id(0)
+def mlp_kernel(x_ref, wg_ref, wu_hbm, wd_hbm, o_ref, wu_buf, wd_buf, sems):
+    steps = wg_ref.shape[2] // H_BLOCK
+
+    def fetch(j):
+        slot = j % 2
+        cols = pl.ds(j * H_BLOCK, H_BLOCK)
+        return (
+            pltpu.make_async_copy(wu_hbm.at[0, :, cols], wu_buf.at[slot], sems.at[0, slot]),
+            pltpu.make_async_copy(wd_hbm.at[0, cols, :], wd_buf.at[slot], sems.at[1, slot]),
+        )
+
     x = x_ref[...]
-    gate_part = jnp.dot(x, wg_ref[...], preferred_element_type=jnp.float32)
-    up_part = jnp.dot(x, wu_ref[...], preferred_element_type=jnp.float32)
-    hidden = (gate_part / (1.0 + jnp.exp(-gate_part)) * up_part).astype(jnp.bfloat16)
-    part = jnp.dot(hidden, wd_ref[...], preferred_element_type=jnp.float32)
-
-    @pl.when(j == 0)
-    def _():
-        acc_ref[...] = part
-
-    @pl.when(j > 0)
-    def _():
-        acc_ref[...] += part
-
-    @pl.when(j == pl.num_programs(0) - 1)
-    def _():
-        o_ref[...] = acc_ref[...].astype(o_ref.dtype)
+    pending = fetch(0)
+    for c in pending:
+        c.start()
+    acc = None
+    for j in range(steps):
+        slot = j % 2
+        current = pending
+        if j + 1 < steps:
+            pending = fetch(j + 1)
+            for c in pending:
+                c.start()
+        for c in current:
+            c.wait()
+        cols = pl.ds(j * H_BLOCK, H_BLOCK)
+        gate_part = jnp.dot(x, wg_ref[0, :, cols], preferred_element_type=jnp.float32)
+        up_part = jnp.dot(x, wu_buf[slot], preferred_element_type=jnp.float32)
+        hidden = (gate_part / (1.0 + jnp.exp(-gate_part)) * up_part).astype(jnp.bfloat16)
+        part = jnp.dot(hidden, wd_buf[slot], preferred_element_type=jnp.float32)
+        acc = part if acc is None else acc + part
+    o_ref[...] = acc.astype(o_ref.dtype)
 
 
 def expert_rows(rows, w_gate, w_up, w_down):
     slots, width = rows.shape
     hid = w_gate.shape[2]
-    steps = hid // H_BLOCK
     cost = pl.CostEstimate(
         flops=6 * slots * width * hid,
         transcendentals=slots * hid,
         bytes_accessed=2 * (3 * width * hid + 2 * slots * width),
     )
+    vmem = pl.BlockSpec(memory_space=pltpu.VMEM)
+    anyspace = pl.BlockSpec(memory_space=pl.ANY)
     return pl.pallas_call(
         mlp_kernel,
-        grid=(steps,),
-        in_specs=[
-            pl.BlockSpec((slots, width), lambda j: (0, 0)),
-            pl.BlockSpec((None, width, H_BLOCK), lambda j: (0, 0, j)),
-            pl.BlockSpec((None, width, H_BLOCK), lambda j: (0, 0, j)),
-            pl.BlockSpec((None, H_BLOCK, width), lambda j: (0, j, 0)),
+        in_specs=[vmem, vmem, anyspace, anyspace],
+        out_specs=vmem,
+        out_shape=jax.ShapeDtypeStruct((slots, width), jnp.bfloat16),
+        scratch_shapes=[
+            pltpu.VMEM((2, width, H_BLOCK), jnp.bfloat16),
+            pltpu.VMEM((2, H_BLOCK, width), jnp.bfloat16),
+            pltpu.SemaphoreType.DMA((2, 2)),
         ],
-        out_specs=pl.BlockSpec((slots, width), lambda j: (0, 0)),
-        out_shape=jax.ShapeDtypeStruct((slots, width), jnp.bfloat16),
-        scratch_shapes=[pltpu.VMEM((slots, width), jnp.float32)],
-        compiler_params=pltpu.CompilerParams(
-            dimension_semantics=("arbitrary",), vmem_limit_bytes=48 * 1024 * 1024
-        ),
+        compiler_params=pltpu.CompilerParams(vmem_limit_bytes=40 * 1024 * 1024),
         cost_estimate=cost,
     )(rows, w_gate, w_up, w_down)
 

time: 91.6 us -> 89 us (0.972)
  Pallas kernels: 11.6 us -> 8.96 us
    pallas_call x1, Pallas kernels: 11.6 us -> 8.96 us  [expert_rows(): pl.pallas_call(mlp_kernel, in_specs=[vmem, vmem, anyspace, anyspace], out...]
where the time goes in v3:
time: 89 us; the launch traced here: 88.8 us
  blocking collectives  38.5 us (43%)
  waiting for transfers between devices  27.1 us (30%)
  Pallas kernels  8.96 us (10%)
  local copies, waits for them, and re-layouts  6.27 us (7%)
  starting transfers between devices  4.95 us (6%)
  matrix products  2.03 us (2%)
    all_to_all x1, blocking collectives, local(): lax.all_to_all(outgoing.reshape(capacity, experts, width), ('group', 'loc...  38.5 us
    all_to_all x1, waiting for transfers between devices, local(): lax.all_to_all(produced.reshape(capacity, experts, width), ('group', 'loc...  27.1 us
    pallas_call x1, Pallas kernels, expert_rows(): pl.pallas_call(mlp_kernel, in_specs=[vmem, vmem, anyspace, anyspace], out...  8.96 us
    all_to_all x1, starting transfers between devices, local(): lax.all_to_all(produced.reshape(capacity, experts, width), ('group', 'loc...  4.95 us
    reshape x1, local copies, waits for them, and re-layouts, local(): produced.reshape(capacity, experts, width)  3.14 us
    reshape x1, local copies, waits for them, and re-layouts, local(): outgoing.reshape(capacity, experts, width)  1.89 us
  transfers between devices with their start and end apart: 1, of which 1 were waited for; matrix products, arithmetic and copies ran while one was open for 0% of the time, Pallas kernels for 0%

profile of v3, /device:TPU:1, one launch (start us, length us, event | category | flops | bytes accessed | tf_op | source)
XLA Modules:
  0.0 88.8 jit_solution(16948558165343183216)
XLA Ops:
  0.0 0.0 copy-start
  0.0 0.8 copy.23
  0.8 0.1 convert_reduce_fusion
  0.9 0.4 select_reduce_fusion.1
  1.4 0.1 fusion.1
  1.5 0.0 copy-done
  1.5 0.7 convolution_convert_fusion
  2.2 1.9 %copy.26 = bf16[2,128,3584]{2,0,1:T(2,128)(2,1)S(1)} copy(bf16[2,128,3584]{2,1,0:T(8,128)(2,1)S(1)} %bitcast.12) | data formatting | bytes 3670016 | tf_op jit(solution)/shard_map/reshape | solution.py:92
  4.1 0.0 copy-start.1
  4.1 38.5 %all_to_all.10 = bf16[2,128,3584]{2,0,1:T(2,128)(2,1)S(1)} all-to-all(bf16[2,128,3584]{2,0,1:T(2,128)(2,1)S(1)} %copy.26), channel_id=1, replica_groups=mesh['group'=16,'local'=8] {'group','local'}, dimensions={1} | all-to-all | bytes 3670016 | tf_op jit(solution)/shard_map/all_to_all | solution.py:91
  42.6 0.2 copy.27
  42.8 0.0 copy-done.1
  42.8 9.0 %shard_map.64 = bf16[256,3584]{1,0:T(8,128)(2,1)S(1)} custom-call(bf16[256,3584]{1,0:T(8,128)(2,1)S(1)} %bitcast.8, bf16[1,3584,1024]{2,1,0:T(8,128)(2,1)S(1)} %copy-done.1, bf16[1,3584,1024]{2,1,0:T(8,128)(2,1)} %wu_hbm.1, bf16[1,1024,3584]{2,1,0:T(8,128)(2,1)} %wd_hbm.1), custom_call_target="tpu_custom_call" | custom-call | flops 5637144576 | bytes 25690112 | tf_op jit(solution)/shard_map/pallas_call | solution.py:55
  51.8 3.1 %copy.28 = bf16[2,128,3584]{2,0,1:T(2,128)(2,1)} copy(bf16[2,128,3584]{2,1,0:T(8,128)(2,1)S(1)} %bitcast.9) | data formatting | bytes 3670016 | tf_op jit(solution)/shard_map/reshape | solution.py:101
  54.9 0.0 copy-start.2
  54.9 5.0 %all-to-all-start.1 = ((bf16[2,128,3584]{2,0,1:T(2,128)(2,1)}), bf16[2,128,3584]{2,0,1:T(2,128)(2,1)S(1)}, u32[]{:S(2)}, u32[]{:S(2)}) async-start(bf16[2,128,3584]{2,0,1:T(2,128)(2,1)} %copy.28), calls=%async_computation.1 | async-start | bytes 3670016 | tf_op jit(solution)/shard_map/all_to_all | solution.py:100
  59.9 0.0 copy-done.2
  59.9 0.1 copy.25
  60.0 0.1 select_reduce_fusion
  60.1 27.1 %all-to-all-done.1 = bf16[2,128,3584]{2,0,1:T(2,128)(2,1)S(1)} async-done(((bf16[2,128,3584]{2,0,1:T(2,128)(2,1)}), bf16[2,128,3584]{2,0,1:T(2,128)(2,1)S(1)}, u32[]{:S(2)}, u32[]{:S(2)}) %all-to-all-start.1) | async-done | bytes 1835040 | tf_op jit(solution)/shard_map/all_to_all | solution.py:100
  87.2 0.2 copy.29
  87.4 0.3 fusion.4
  87.8 1.0 %fusion = bf16[16,3584]{1,0:T(8,128)(2,1)} fusion(f32[16,3584]{1,0:T(8,128)S(1)} %fusion.4, bf16[256,3584]{1,0:T(8,128)(2,1)S(1)} %bitcast.11, f32[16,256]{1,0:T(8,128)S(1)} %select_reduce_fusion), kind=kOutput, calls=%fused_computation.2 | convolution fusion | flops 29487104 | bytes 2195456 | tf_op jit(solution)/shard_map/dot_general | solution.py:114
  (4 shorter events, 0.1 us)
Async XLA Ops:
  0.0 1.5 %copy-start = (bf16[16,3584]{1,0:T(8,128)(2,1)S(1)}, bf16[16,3584]{1,0:T(8,128)(2,1)}, u32[]{:S(2)}) copy-start(bf16[16,3584]{1,0:T(8,128)(2,1)} %param.6) | copy-start | bytes 344068
  4.1 38.7 %copy-start.1 = (bf16[1,3584,1024]{2,1,0:T(8,128)(2,1)S(1)}, bf16[1,3584,1024]{2,1,0:T(8,128)(2,1)}, u32[]{:S(2)}) copy-start(bf16[1,3584,1024]{2,1,0:T(8,128)(2,1)} %wg_ref.1) | copy-start | bytes 22020100
  54.9 5.0 %copy-start.2 = (s32[16,8]{0,1:T(8,128)S(1)}, s32[16,8]{0,1:T(8,128)}, u32[]{:S(2)}) copy-start(s32[16,8]{0,1:T(8,128)} %param.8) | copy-start | bytes 1540
  54.9 32.3 %all-to-all-start.1 = ((bf16[2,128,3584]{2,0,1:T(2,128)(2,1)}), bf16[2,128,3584]{2,0,1:T(2,128)(2,1)S(1)}, u32[]{:S(2)}, u32[]{:S(2)}) async-start(bf16[2,128,3584]{2,0,1:T(2,128)(2,1)} %copy.28), calls=%async_computation.1 | async-start | bytes 3670016 | tf_op jit(solution)/shard_map/all_to_all | solution.py:100

commit v4 on v3

--- a/solution.py
+++ b/solution.py
@@ -39,7 +39,9 @@
         hidden = (gate_part / (1.0 + jnp.exp(-gate_part)) * up_part).astype(jnp.bfloat16)
         part = jnp.dot(hidden, wd_buf[slot], preferred_element_type=jnp.float32)
         acc = part if acc is None else acc + part
-    o_ref[...] = acc.astype(o_ref.dtype)
+    half = acc.shape[0] // 2
+    for r in range(2):
+        o_ref[:, r, :] = acc[r * half:(r + 1) * half].astype(o_ref.dtype)
 
 
 def expert_rows(rows, w_gate, w_up, w_down):
@@ -56,7 +58,7 @@
         mlp_kernel,
         in_specs=[vmem, vmem, anyspace, anyspace],
         out_specs=vmem,
-        out_shape=jax.ShapeDtypeStruct((slots, width), jnp.bfloat16),
+        out_shape=jax.ShapeDtypeStruct((slots // 2, 2, width), jnp.bfloat16),
         scratch_shapes=[
             pltpu.VMEM((2, width, H_BLOCK), jnp.bfloat16),
             pltpu.VMEM((2, H_BLOCK, width), jnp.bfloat16),
@@ -97,14 +99,8 @@
     )
     rows_in = got_rows.reshape(total_slots, width)
     produced = expert_rows(rows_in, w_gate, w_up, w_down)
-    returned = lax.all_to_all(
-        produced.reshape(capacity, experts, width),
-        ("group", "local"),
-        split_axis=1,
-        concat_axis=1,
-        tiled=True,
-    )
-    back_flat = returned.reshape(total_slots, width)
+    returned = lax.all_to_all(produced, ("group", "local"), split_axis=0, concat_axis=0, tiled=True)
+    back_flat = jnp.swapaxes(returned, 0, 1).reshape(total_slots, width)
     weight = jnp.where(kept, gate_codes.astype(jnp.float32) / 1024.0, jnp.zeros((), jnp.float32))
     combine = jnp.sum(jnp.where(route_hit, weight[:, :, None], 0.0), axis=1)
     combine_hi = lax.reduce_precision(combine, exponent_bits=8, mantissa_bits=7)

time: 89 us -> 87.6 us (0.984)
  local copies, waits for them, and re-layouts: 6.27 us -> 3.13 us
  Pallas kernels: 8.96 us -> 10.8 us
    reshape x1 -> x0, local copies, waits for them, and re-layouts: 3.14 us -> none  [local(): produced.reshape(capacity, experts, width)]
    pallas_call x1, Pallas kernels: 8.96 us -> 10.8 us  [expert_rows(): pl.pallas_call(mlp_kernel, in_specs=[vmem, vmem, anyspace, anyspace], out...]
where the time goes in v4:
time: 87.6 us; the launch traced here: 87.3 us
  blocking collectives  38.5 us (44%)
  waiting for transfers between devices  27.1 us (31%)
  Pallas kernels  10.8 us (12%)
  starting transfers between devices  4.83 us (6%)
  local copies, waits for them, and re-layouts  3.13 us (4%)
  matrix products  2.03 us (2%)
    all_to_all x1, blocking collectives, local(): lax.all_to_all(outgoing.reshape(capacity, experts, width), ('group', 'loc...  38.5 us
    all_to_all x1, waiting for transfers between devices, local(): lax.all_to_all(produced, ('group', 'local'), split_axis=0, concat_axis=0,...  27.1 us
    pallas_call x1, Pallas kernels, expert_rows(): pl.pallas_call(mlp_kernel, in_specs=[vmem, vmem, anyspace, anyspace], out...  10.8 us
    all_to_all x1, starting transfers between devices, local(): lax.all_to_all(produced, ('group', 'local'), split_axis=0, concat_axis=0,...  4.83 us
    reshape x1, local copies, waits for them, and re-layouts, local(): outgoing.reshape(capacity, experts, width)  1.89 us
  transfers between devices with their start and end apart: 1, of which 1 were waited for; matrix products, arithmetic and copies ran while one was open for 0% of the time, Pallas kernels for 0%

profile of v4, /device:TPU:1, one launch (start us, length us, event | category | flops | bytes accessed | tf_op | source)
XLA Modules:
  0.0 87.3 jit_solution(6411808237898212077)
XLA Ops:
  0.0 0.0 copy-start
  0.0 0.8 copy.20
  0.8 0.1 convert_reduce_fusion
  0.9 0.4 select_reduce_fusion.1
  1.4 0.1 fusion.1
  1.5 0.0 copy-done
  1.5 0.7 convolution_convert_fusion
  2.2 1.9 %copy.23 = bf16[2,128,3584]{2,0,1:T(2,128)(2,1)S(1)} copy(bf16[2,128,3584]{2,1,0:T(8,128)(2,1)S(1)} %bitcast.12) | data formatting | bytes 3670016 | tf_op jit(solution)/shard_map/reshape | solution.py:94
  4.1 0.0 copy-start.1
  4.1 38.5 %all_to_all.10 = bf16[2,128,3584]{2,0,1:T(2,128)(2,1)S(1)} all-to-all(bf16[2,128,3584]{2,0,1:T(2,128)(2,1)S(1)} %copy.23), channel_id=1, replica_groups=mesh['group'=16,'local'=8] {'group','local'}, dimensions={1} | all-to-all | bytes 3670016 | tf_op jit(solution)/shard_map/all_to_all | solution.py:93
  42.6 0.2 copy.24
  42.8 0.0 copy-done.1
  42.8 10.8 %shard_map.64 = bf16[128,2,3584]{2,1,0:T(2,128)(2,1)} custom-call(bf16[256,3584]{1,0:T(8,128)(2,1)S(1)} %bitcast.8, bf16[1,3584,1024]{2,1,0:T(8,128)(2,1)S(1)} %copy-done.1, bf16[1,3584,1024]{2,1,0:T(8,128)(2,1)} %wu_hbm.1, bf16[1,1024,3584]{2,1,0:T(8,128)(2,1)} %wd_hbm.1), custom_call_target="tpu_custom_call" | custom-call | flops 5637144576 | bytes 25690112 | tf_op jit(solution)/shard_map/pallas_call | solution.py:57
  53.6 0.0 copy-start.2
  53.6 4.8 %all-to-all-start.1 = ((bf16[128,2,3584]{2,1,0:T(2,128)(2,1)}), bf16[128,2,3584]{2,1,0:T(2,128)(2,1)S(1)}, u32[]{:S(2)}, u32[]{:S(2)}) async-start(bf16[128,2,3584]{2,1,0:T(2,128)(2,1)} %shard_map.64), calls=%async_computation.1 | async-start | bytes 3670016 | tf_op jit(solution)/shard_map/all_to_all | solution.py:102
  58.4 0.0 copy-done.2
  58.4 0.1 copy.22
  58.5 0.1 select_reduce_fusion
  58.7 27.1 %all-to-all-done.1 = bf16[128,2,3584]{2,1,0:T(2,128)(2,1)S(1)} async-done(((bf16[128,2,3584]{2,1,0:T(2,128)(2,1)}), bf16[128,2,3584]{2,1,0:T(2,128)(2,1)S(1)}, u32[]{:S(2)}, u32[]{:S(2)}) %all-to-all-start.1) | async-done | bytes 1835040 | tf_op jit(solution)/shard_map/all_to_all | solution.py:102
  85.8 0.2 copy.25
  86.0 0.3 fusion.4
  86.3 1.0 %fusion = bf16[16,3584]{1,0:T(8,128)(2,1)} fusion(f32[16,3584]{1,0:T(8,128)S(1)} %fusion.4, bf16[256,3584]{1,0:T(8,128)(2,1)S(1)} %bitcast.10, f32[16,256]{1,0:T(8,128)S(1)} %select_reduce_fusion), kind=kOutput, calls=%fused_computation.2 | convolution fusion | flops 29487104 | bytes 2195456 | tf_op jit(solution)/shard_map/dot_general | solution.py:110
  (4 shorter events, 0.1 us)
Async XLA Ops:
  0.0 1.5 %copy-start = (bf16[16,3584]{1,0:T(8,128)(2,1)S(1)}, bf16[16,3584]{1,0:T(8,128)(2,1)}, u32[]{:S(2)}) copy-start(bf16[16,3584]{1,0:T(8,128)(2,1)} %param.6) | copy-start | bytes 344068
  4.1 38.7 %copy-start.1 = (bf16[1,3584,1024]{2,1,0:T(8,128)(2,1)S(1)}, bf16[1,3584,1024]{2,1,0:T(8,128)(2,1)}, u32[]{:S(2)}) copy-start(bf16[1,3584,1024]{2,1,0:T(8,128)(2,1)} %wg_ref.1) | copy-start | bytes 22020100
  53.6 4.9 %copy-start.2 = (s32[16,8]{0,1:T(8,128)S(1)}, s32[16,8]{0,1:T(8,128)}, u32[]{:S(2)}) copy-start(s32[16,8]{0,1:T(8,128)} %param.8) | copy-start | bytes 1540
  53.6 32.2 %all-to-all-start.1 = ((bf16[128,2,3584]{2,1,0:T(2,128)(2,1)}), bf16[128,2,3584]{2,1,0:T(2,128)(2,1)S(1)}, u32[]{:S(2)}, u32[]{:S(2)}) async-start(bf16[128,2,3584]{2,1,0:T(2,128)(2,1)} %shard_map.64), calls=%async_computation.1 | async-start | bytes 3670016 | tf_op jit(solution)/shard_map/all_to_all | solution.py:102

commit v5 on v4

--- a/solution.py
+++ b/solution.py
@@ -69,6 +69,26 @@
     )(rows, w_gate, w_up, w_down)
 
 
+def build_kernel(pick_ref, tok_ref, o_ref):
+    tokens = tok_ref[...]
+    for r in range(o_ref.shape[1]):
+        o_ref[:, r, :] = jnp.dot(
+            pick_ref[r], tokens, preferred_element_type=jnp.float32
+        ).astype(o_ref.dtype)
+
+
+def build_rows(pick, tokens):
+    ranks, experts, _ = pick.shape
+    vmem = pl.BlockSpec(memory_space=pltpu.VMEM)
+    return pl.pallas_call(
+        build_kernel,
+        in_specs=[vmem, vmem],
+        out_specs=vmem,
+        out_shape=jax.ShapeDtypeStruct((experts, ranks, tokens.shape[1]), tokens.dtype),
+        compiler_params=pltpu.CompilerParams(vmem_limit_bytes=2 * 1024 * 1024),
+    )(pick, tokens)
+
+
 def local(tokens, expert_ids, gate_codes, w_gate, w_up, w_down):
     tok_rows, width = tokens.shape
     top = expert_ids.shape[1]
@@ -87,17 +107,9 @@
     slot_range = jnp.arange(total_slots, dtype=jnp.int32)
     route_hit = slot_index[:, :, None] == slot_range[None, None, :]
     pick = jnp.any(route_hit, axis=1)
-    outgoing = jnp.dot(
-        pick.T.astype(jnp.bfloat16), tokens, preferred_element_type=jnp.float32
-    ).astype(jnp.bfloat16)
-    got_rows = lax.all_to_all(
-        outgoing.reshape(capacity, experts, width),
-        ("group", "local"),
-        split_axis=1,
-        concat_axis=1,
-        tiled=True,
-    )
-    rows_in = got_rows.reshape(total_slots, width)
+    outgoing = build_rows(pick.T.astype(jnp.bfloat16).reshape(capacity, experts, tok_rows), tokens)
+    got_rows = lax.all_to_all(outgoing, ("group", "local"), split_axis=0, concat_axis=0, tiled=True)
+    rows_in = jnp.swapaxes(got_rows, 0, 1).reshape(total_slots, width)
     produced = expert_rows(rows_in, w_gate, w_up, w_down)
     returned = lax.all_to_all(produced, ("group", "local"), split_axis=0, concat_axis=0, tiled=True)
     back_flat = jnp.swapaxes(returned, 0, 1).reshape(total_slots, width)

time: 87.6 us -> 86.9 us (level)
  local copies, waits for them, and re-layouts: 3.13 us -> 2.22 us
  Pallas kernels: 10.8 us -> 11.7 us
    reshape x1, local copies, waits for them, and re-layouts: 1.89 us -> 0.12 us  [local(): pick.T.astype(jnp.bfloat16).reshape(capacity, experts, tok_rows)]
    pallas_call x0 -> x1, Pallas kernels: none -> 0.88 us  [build_rows(): pl.pallas_call(build_kernel, in_specs=[vmem, vmem], out_specs=vmem, out_s...]
where the time goes in v5:
time: 86.9 us; the launch traced here: 86.6 us
  blocking collectives  38.5 us (44%)
  waiting for transfers between devices  27.1 us (31%)
  Pallas kernels  11.7 us (13%)
  starting transfers between devices  4.82 us (6%)
  local copies, waits for them, and re-layouts  2.22 us (3%)
  matrix products  1.36 us (2%)
    all_to_all x1, blocking collectives, local(): lax.all_to_all(outgoing, ('group', 'local'), split_axis=0, concat_axis=0,...  38.5 us
    all_to_all x1, waiting for transfers between devices, local(): lax.all_to_all(produced, ('group', 'local'), split_axis=0, concat_axis=0,...  27.1 us
    pallas_call x1, Pallas kernels, expert_rows(): pl.pallas_call(mlp_kernel, in_specs=[vmem, vmem, anyspace, anyspace], out...  10.8 us
    all_to_all x1, starting transfers between devices, local(): lax.all_to_all(produced, ('group', 'local'), split_axis=0, concat_axis=0,...  4.82 us
  transfers between devices with their start and end apart: 1, of which 1 were waited for; matrix products, arithmetic and copies ran while one was open for 0% of the time, Pallas kernels for 0%

profile of v5, /device:TPU:1, one launch (start us, length us, event | category | flops | bytes accessed | tf_op | source)
XLA Modules:
  0.0 86.6 jit_solution(6114596470963772377)
XLA Ops:
  0.0 0.8 copy.16
  0.8 0.1 convert_reduce_fusion
  0.9 0.4 select_reduce_fusion.1
  1.3 0.1 fusion.1
  1.5 0.1 copy.19
  1.6 0.0 copy-start.1
  1.6 0.9 %copy-done.1 = bf16[16,3584]{1,0:T(8,128)(2,1)S(1)} copy-done((bf16[16,3584]{1,0:T(8,128)(2,1)S(1)}, bf16[16,3584]{1,0:T(8,128)(2,1)}, u32[]{:S(2)}) %copy-start.1) | copy-done | bytes 114712
  2.5 0.9 %shard_map.64 = bf16[128,2,3584]{2,1,0:T(2,128)(2,1)S(1)} custom-call(bf16[2,128,16]{2,1,0:T(8,128)(2,1)S(1)} %bitcast.10, bf16[16,3584]{1,0:T(8,128)(2,1)S(1)} %copy-done.1), custom_call_target="tpu_custom_call" | custom-call | tf_op jit(solution)/shard_map/pallas_call | solution.py:83
  3.4 0.0 copy-start
  3.4 38.5 %all_to_all.10 = bf16[128,2,3584]{2,1,0:T(2,128)(2,1)S(1)} all-to-all(bf16[128,2,3584]{2,1,0:T(2,128)(2,1)S(1)} %shard_map.64), channel_id=1, replica_groups=mesh['group'=16,'local'=8] {'group','local'}, dimensions={0} | all-to-all | bytes 3670016 | tf_op jit(solution)/shard_map/all_to_all | solution.py:111
  41.9 0.2 copy.20
  42.1 0.0 copy-done
  42.1 10.8 %shard_map.65 = bf16[128,2,3584]{2,1,0:T(2,128)(2,1)} custom-call(bf16[256,3584]{1,0:T(8,128)(2,1)S(1)} %bitcast.9, bf16[1,3584,1024]{2,1,0:T(8,128)(2,1)S(1)} %copy-done, bf16[1,3584,1024]{2,1,0:T(8,128)(2,1)} %wu_hbm.1, bf16[1,1024,3584]{2,1,0:T(8,128)(2,1)} %wd_hbm.1), custom_call_target="tpu_custom_call" | custom-call | flops 5637144576 | bytes 25690112 | tf_op jit(solution)/shard_map/pallas_call | solution.py:57
  52.9 0.0 copy-start.2
  52.9 4.8 %all-to-all-start.1 = ((bf16[128,2,3584]{2,1,0:T(2,128)(2,1)}), bf16[128,2,3584]{2,1,0:T(2,128)(2,1)S(1)}, u32[]{:S(2)}, u32[]{:S(2)}) async-start(bf16[128,2,3584]{2,1,0:T(2,128)(2,1)} %shard_map.65), calls=%async_computation.1 | async-start | bytes 3670016 | tf_op jit(solution)/shard_map/all_to_all | solution.py:114
  57.7 0.0 copy-done.2
  57.7 0.1 copy.18
  57.8 0.1 select_reduce_fusion
  57.9 27.1 %all-to-all-done.1 = bf16[128,2,3584]{2,1,0:T(2,128)(2,1)S(1)} async-done(((bf16[128,2,3584]{2,1,0:T(2,128)(2,1)}), bf16[128,2,3584]{2,1,0:T(2,128)(2,1)S(1)}, u32[]{:S(2)}, u32[]{:S(2)}) %all-to-all-start.1) | async-done | bytes 1835040 | tf_op jit(solution)/shard_map/all_to_all | solution.py:114
  85.1 0.2 copy.21
  85.3 0.3 fusion.4
  85.6 1.0 %fusion = bf16[16,3584]{1,0:T(8,128)(2,1)} fusion(f32[16,3584]{1,0:T(8,128)S(1)} %fusion.4, bf16[256,3584]{1,0:T(8,128)(2,1)S(1)} %bitcast.12, f32[16,256]{1,0:T(8,128)S(1)} %select_reduce_fusion), kind=kOutput, calls=%fused_computation.1 | convolution fusion | flops 29487104 | bytes 2195456 | tf_op jit(solution)/shard_map/dot_general | solution.py:122
  (5 shorter events, 0.1 us)
Async XLA Ops:
  1.6 0.9 %copy-start.1 = (bf16[16,3584]{1,0:T(8,128)(2,1)S(1)}, bf16[16,3584]{1,0:T(8,128)(2,1)}, u32[]{:S(2)}) copy-start(bf16[16,3584]{1,0:T(8,128)(2,1)} %tok_ref.1) | copy-start | bytes 344068
  3.4 38.7 %copy-start = (bf16[1,3584,1024]{2,1,0:T(8,128)(2,1)S(1)}, bf16[1,3584,1024]{2,1,0:T(8,128)(2,1)}, u32[]{:S(2)}) copy-start(bf16[1,3584,1024]{2,1,0:T(8,128)(2,1)} %wg_ref.1) | copy-start | bytes 22020100
  52.9 4.8 %copy-start.2 = (s32[16,8]{0,1:T(8,128)S(1)}, s32[16,8]{0,1:T(8,128)}, u32[]{:S(2)}) copy-start(s32[16,8]{0,1:T(8,128)} %param.8) | copy-start | bytes 1540
  52.9 32.2 %all-to-all-start.1 = ((bf16[128,2,3584]{2,1,0:T(2,128)(2,1)}), bf16[128,2,3584]{2,1,0:T(2,128)(2,1)S(1)}, u32[]{:S(2)}, u32[]{:S(2)}) async-start(bf16[128,2,3584]{2,1,0:T(2,128)(2,1)} %shard_map.65), calls=%async_computation.1 | async-start | bytes 3670016 | tf_op jit(solution)/shard_map/all_to_all | solution.py:114

commit v6 on v5

--- a/solution.py
+++ b/solution.py
@@ -23,6 +23,7 @@
     pending = fetch(0)
     for c in pending:
         c.start()
+    gate_all = jnp.dot(x, wg_ref[0], preferred_element_type=jnp.float32)
     acc = None
     for j in range(steps):
         slot = j % 2
@@ -33,8 +34,7 @@
                 c.start()
         for c in current:
             c.wait()
-        cols = pl.ds(j * H_BLOCK, H_BLOCK)
-        gate_part = jnp.dot(x, wg_ref[0, :, cols], preferred_element_type=jnp.float32)
+        gate_part = gate_all[:, j * H_BLOCK:(j + 1) * H_BLOCK]
         up_part = jnp.dot(x, wu_buf[slot], preferred_element_type=jnp.float32)
         hidden = (gate_part / (1.0 + jnp.exp(-gate_part)) * up_part).astype(jnp.bfloat16)
         part = jnp.dot(hidden, wd_buf[slot], preferred_element_type=jnp.float32)

time: 86.9 us -> 87.9 us (1.012)
  Pallas kernels: 11.7 us -> 12.6 us
    pallas_call x1, Pallas kernels: 10.8 us -> 11.8 us  [expert_rows(): pl.pallas_call(mlp_kernel, in_specs=[vmem, vmem, anyspace, anyspace], out...]
where the time goes in v6:
time: 87.9 us; the launch traced here: 87.6 us
  blocking collectives  38.5 us (44%)
  waiting for transfers between devices  27.1 us (31%)
  Pallas kernels  12.6 us (14%)
  starting transfers between devices  4.83 us (5%)
  local copies, waits for them, and re-layouts  2.22 us (3%)
  matrix products  1.36 us (2%)
    all_to_all x1, blocking collectives, local(): lax.all_to_all(outgoing, ('group', 'local'), split_axis=0, concat_axis=0,...  38.5 us
    all_to_all x1, waiting for transfers between devices, local(): lax.all_to_all(produced, ('group', 'local'), split_axis=0, concat_axis=0,...  27.1 us
    pallas_call x1, Pallas kernels, expert_rows(): pl.pallas_call(mlp_kernel, in_specs=[vmem, vmem, anyspace, anyspace], out...  11.8 us
    all_to_all x1, starting transfers between devices, local(): lax.all_to_all(produced, ('group', 'local'), split_axis=0, concat_axis=0,...  4.83 us
  transfers between devices with their start and end apart: 1, of which 1 were waited for; matrix products, arithmetic and copies ran while one was open for 0% of the time, Pallas kernels for 0%

profile of v6, /device:TPU:1, one launch (start us, length us, event | category | flops | bytes accessed | tf_op | source)
XLA Modules:
  0.0 87.6 jit_solution(62718889397362670)
XLA Ops:
  0.0 0.8 copy.16
  0.8 0.1 convert_reduce_fusion
  0.9 0.4 select_reduce_fusion.1
  1.3 0.1 fusion.1
  1.5 0.1 copy.19
  1.6 0.0 copy-start.1
  1.6 0.9 %copy-done.1 = bf16[16,3584]{1,0:T(8,128)(2,1)S(1)} copy-done((bf16[16,3584]{1,0:T(8,128)(2,1)S(1)}, bf16[16,3584]{1,0:T(8,128)(2,1)}, u32[]{:S(2)}) %copy-start.1) | copy-done | bytes 114712
  2.5 0.9 %shard_map.64 = bf16[128,2,3584]{2,1,0:T(2,128)(2,1)S(1)} custom-call(bf16[2,128,16]{2,1,0:T(8,128)(2,1)S(1)} %bitcast.10, bf16[16,3584]{1,0:T(8,128)(2,1)S(1)} %copy-done.1), custom_call_target="tpu_custom_call" | custom-call | tf_op jit(solution)/shard_map/pallas_call | solution.py:83
  3.4 0.0 copy-start
  3.4 38.5 %all_to_all.10 = bf16[128,2,3584]{2,1,0:T(2,128)(2,1)S(1)} all-to-all(bf16[128,2,3584]{2,1,0:T(2,128)(2,1)S(1)} %shard_map.64), channel_id=1, replica_groups=mesh['group'=16,'local'=8] {'group','local'}, dimensions={0} | all-to-all | bytes 3670016 | tf_op jit(solution)/shard_map/all_to_all | solution.py:111
  41.9 0.2 copy.20
  42.1 0.0 copy-done
  42.1 11.8 %shard_map.65 = bf16[128,2,3584]{2,1,0:T(2,128)(2,1)} custom-call(bf16[256,3584]{1,0:T(8,128)(2,1)S(1)} %bitcast.9, bf16[1,3584,1024]{2,1,0:T(8,128)(2,1)S(1)} %copy-done, bf16[1,3584,1024]{2,1,0:T(8,128)(2,1)} %wu_hbm.1, bf16[1,1024,3584]{2,1,0:T(8,128)(2,1)} %wd_hbm.1), custom_call_target="tpu_custom_call" | custom-call | flops 5637144576 | bytes 25690112 | tf_op jit(solution)/shard_map/pallas_call | solution.py:57
  53.9 0.0 copy-start.2
  53.9 4.8 %all-to-all-start.1 = ((bf16[128,2,3584]{2,1,0:T(2,128)(2,1)}), bf16[128,2,3584]{2,1,0:T(2,128)(2,1)S(1)}, u32[]{:S(2)}, u32[]{:S(2)}) async-start(bf16[128,2,3584]{2,1,0:T(2,128)(2,1)} %shard_map.65), calls=%async_computation.1 | async-start | bytes 3670016 | tf_op jit(solution)/shard_map/all_to_all | solution.py:114
  58.7 0.0 copy-done.2
  58.7 0.1 copy.18
  58.8 0.1 select_reduce_fusion
  58.9 27.1 %all-to-all-done.1 = bf16[128,2,3584]{2,1,0:T(2,128)(2,1)S(1)} async-done(((bf16[128,2,3584]{2,1,0:T(2,128)(2,1)}), bf16[128,2,3584]{2,1,0:T(2,128)(2,1)S(1)}, u32[]{:S(2)}, u32[]{:S(2)}) %all-to-all-start.1) | async-done | bytes 1835040 | tf_op jit(solution)/shard_map/all_to_all | solution.py:114
  86.1 0.2 copy.21
  86.3 0.3 fusion.4
  86.6 1.0 %fusion = bf16[16,3584]{1,0:T(8,128)(2,1)} fusion(f32[16,3584]{1,0:T(8,128)S(1)} %fusion.4, bf16[256,3584]{1,0:T(8,128)(2,1)S(1)} %bitcast.12, f32[16,256]{1,0:T(8,128)S(1)} %select_reduce_fusion), kind=kOutput, calls=%fused_computation.1 | convolution fusion | flops 29487104 | bytes 2195456 | tf_op jit(solution)/shard_map/dot_general | solution.py:122
  (5 shorter events, 0.1 us)
Async XLA Ops:
  1.6 0.9 %copy-start.1 = (bf16[16,3584]{1,0:T(8,128)(2,1)S(1)}, bf16[16,3584]{1,0:T(8,128)(2,1)}, u32[]{:S(2)}) copy-start(bf16[16,3584]{1,0:T(8,128)(2,1)} %tok_ref.1) | copy-start | bytes 344068
  3.4 38.7 %copy-start = (bf16[1,3584,1024]{2,1,0:T(8,128)(2,1)S(1)}, bf16[1,3584,1024]{2,1,0:T(8,128)(2,1)}, u32[]{:S(2)}) copy-start(bf16[1,3584,1024]{2,1,0:T(8,128)(2,1)} %wg_ref.1) | copy-start | bytes 22020100
  53.9 4.8 %copy-start.2 = (s32[16,8]{0,1:T(8,128)S(1)}, s32[16,8]{0,1:T(8,128)}, u32[]{:S(2)}) copy-start(s32[16,8]{0,1:T(8,128)} %param.8) | copy-start | bytes 1540
  53.9 32.2 %all-to-all-start.1 = ((bf16[128,2,3584]{2,1,0:T(2,128)(2,1)}), bf16[128,2,3584]{2,1,0:T(2,128)(2,1)S(1)}, u32[]{:S(2)}, u32[]{:S(2)}) async-start(bf16[128,2,3584]{2,1,0:T(2,128)(2,1)} %shard_map.65), calls=%async_computation.1 | async-start | bytes 3670016 | tf_op jit(solution)/shard_map/all_to_all | solution.py:114

commit v7 on v5

--- a/solution.py
+++ b/solution.py
@@ -8,37 +8,36 @@
 H_BLOCK = 256
 
 
-def mlp_kernel(x_ref, wg_ref, wu_hbm, wd_hbm, o_ref, wu_buf, wd_buf, sems):
+def mlp_kernel(x_ref, wg_ref, wu_hbm, wd_hbm, o_ref, wu_buf, wd_all, hid_ref, sems):
     steps = wg_ref.shape[2] // H_BLOCK
 
-    def fetch(j):
-        slot = j % 2
+    def fetch_up(j):
         cols = pl.ds(j * H_BLOCK, H_BLOCK)
-        return (
-            pltpu.make_async_copy(wu_hbm.at[0, :, cols], wu_buf.at[slot], sems.at[0, slot]),
-            pltpu.make_async_copy(wd_hbm.at[0, cols, :], wd_buf.at[slot], sems.at[1, slot]),
-        )
+        return pltpu.make_async_copy(wu_hbm.at[0, :, cols], wu_buf.at[j % 2], sems.at[0, j % 2])
+
+    def fetch_down(j):
+        rows = pl.ds(j * H_BLOCK, H_BLOCK)
+        return pltpu.make_async_copy(wd_hbm.at[0, rows, :], wd_all.at[rows, :], sems.at[1, j])
 
     x = x_ref[...]
-    pending = fetch(0)
-    for c in pending:
-        c.start()
-    acc = None
+    up_next = fetch_up(0)
+    up_next.start()
+    downs = []
     for j in range(steps):
-        slot = j % 2
-        current = pending
+        up_now = up_next
         if j + 1 < steps:
-            pending = fetch(j + 1)
-            for c in pending:
-                c.start()
-        for c in current:
-            c.wait()
+            up_next = fetch_up(j + 1)
+            up_next.start()
+        downs.append(fetch_down(j))
+        downs[-1].start()
+        up_now.wait()
         cols = pl.ds(j * H_BLOCK, H_BLOCK)
         gate_part = jnp.dot(x, wg_ref[0, :, cols], preferred_element_type=jnp.float32)
-        up_part = jnp.dot(x, wu_buf[slot], preferred_element_type=jnp.float32)
-        hidden = (gate_part / (1.0 + jnp.exp(-gate_part)) * up_part).astype(jnp.bfloat16)
-        part = jnp.dot(hidden, wd_buf[slot], preferred_element_type=jnp.float32)
-        acc = part if acc is None else acc + part
+        up_part = jnp.dot(x, wu_buf[j % 2], preferred_element_type=jnp.float32)
+        hid_ref[:, cols] = (gate_part / (1.0 + jnp.exp(-gate_part)) * up_part).astype(jnp.bfloat16)
+    for c in downs:
+        c.wait()
+    acc = jnp.dot(hid_ref[...], wd_all[...], preferred_element_type=jnp.float32)
     half = acc.shape[0] // 2
     for r in range(2):
         o_ref[:, r, :] = acc[r * half:(r + 1) * half].astype(o_ref.dtype)
@@ -61,8 +60,9 @@
         out_shape=jax.ShapeDtypeStruct((slots // 2, 2, width), jnp.bfloat16),
         scratch_shapes=[
             pltpu.VMEM((2, width, H_BLOCK), jnp.bfloat16),
-            pltpu.VMEM((2, H_BLOCK, width), jnp.bfloat16),
-            pltpu.SemaphoreType.DMA((2, 2)),
+            pltpu.VMEM((hid, width), jnp.bfloat16),
+            pltpu.VMEM((slots, hid), jnp.bfloat16),
+            pltpu.SemaphoreType.DMA((2, hid // H_BLOCK)),
         ],
         compiler_params=pltpu.CompilerParams(vmem_limit_bytes=40 * 1024 * 1024),
         cost_estimate=cost,

time: 86.9 us -> 86.2 us (level)
  no operation moved by 1% of the time
where the time goes in v7:
time: 86.2 us; the launch traced here: 86 us
  blocking collectives  38.5 us (45%)
  waiting for transfers between devices  27.1 us (31%)
  Pallas kernels  11 us (13%)
  starting transfers between devices  4.81 us (6%)
  local copies, waits for them, and re-layouts  2.22 us (3%)
  matrix products  1.36 us (2%)
    all_to_all x1, blocking collectives, local(): lax.all_to_all(outgoing, ('group', 'local'), split_axis=0, concat_axis=0,...  38.5 us
    all_to_all x1, waiting for transfers between devices, local(): lax.all_to_all(produced, ('group', 'local'), split_axis=0, concat_axis=0,...  27.1 us
    pallas_call x1, Pallas kernels, expert_rows(): pl.pallas_call(mlp_kernel, in_specs=[vmem, vmem, anyspace, anyspace], out...  10.1 us
    all_to_all x1, starting transfers between devices, local(): lax.all_to_all(produced, ('group', 'local'), split_axis=0, concat_axis=0,...  4.81 us
    unnamed x8, local copies, waits for them, and re-layouts  1.74 us
  transfers between devices with their start and end apart: 1, of which 1 were waited for; matrix products, arithmetic and copies ran while one was open for 0% of the time, Pallas kernels for 0%

profile of v7, /device:TPU:1, one launch (start us, length us, event | category | flops | bytes accessed | tf_op | source)
XLA Modules:
  0.0 86.0 jit_solution(6013208533371946337)
XLA Ops:
  0.0 0.8 copy.16
  0.8 0.1 convert_reduce_fusion
  0.9 0.4 select_reduce_fusion.1
  1.3 0.1 fusion.1
  1.5 0.1 copy.19
  1.6 0.0 copy-start.1
  1.6 0.9 %copy-done.1 = bf16[16,3584]{1,0:T(8,128)(2,1)S(1)} copy-done((bf16[16,3584]{1,0:T(8,128)(2,1)S(1)}, bf16[16,3584]{1,0:T(8,128)(2,1)}, u32[]{:S(2)}) %copy-start.1) | copy-done | bytes 114712
  2.5 0.9 %shard_map.64 = bf16[128,2,3584]{2,1,0:T(2,128)(2,1)S(1)} custom-call(bf16[2,128,16]{2,1,0:T(8,128)(2,1)S(1)} %bitcast.10, bf16[16,3584]{1,0:T(8,128)(2,1)S(1)} %copy-done.1), custom_call_target="tpu_custom_call" | custom-call | tf_op jit(solution)/shard_map/pallas_call | solution.py:83
  3.4 0.0 copy-start
  3.4 38.5 %all_to_all.10 = bf16[128,2,3584]{2,1,0:T(2,128)(2,1)S(1)} all-to-all(bf16[128,2,3584]{2,1,0:T(2,128)(2,1)S(1)} %shard_map.64), channel_id=1, replica_groups=mesh['group'=16,'local'=8] {'group','local'}, dimensions={0} | all-to-all | bytes 3670016 | tf_op jit(solution)/shard_map/all_to_all | solution.py:111
  41.9 0.2 copy.20
  42.1 0.0 copy-done
  42.1 10.1 %shard_map.65 = bf16[128,2,3584]{2,1,0:T(2,128)(2,1)} custom-call(bf16[256,3584]{1,0:T(8,128)(2,1)S(1)} %bitcast.9, bf16[1,3584,1024]{2,1,0:T(8,128)(2,1)S(1)} %copy-done, bf16[1,3584,1024]{2,1,0:T(8,128)(2,1)} %wu_hbm.1, bf16[1,1024,3584]{2,1,0:T(8,128)(2,1)} %wd_hbm.1), custom_call_target="tpu_custom_call" | custom-call | flops 5637144576 | bytes 25690112 | tf_op jit(solution)/shard_map/pallas_call | solution.py:56
  52.2 0.0 copy-start.2
  52.2 4.8 %all-to-all-start.1 = ((bf16[128,2,3584]{2,1,0:T(2,128)(2,1)}), bf16[128,2,3584]{2,1,0:T(2,128)(2,1)S(1)}, u32[]{:S(2)}, u32[]{:S(2)}) async-start(bf16[128,2,3584]{2,1,0:T(2,128)(2,1)} %shard_map.65), calls=%async_computation.1 | async-start | bytes 3670016 | tf_op jit(solution)/shard_map/all_to_all | solution.py:114
  57.1 0.0 copy-done.2
  57.1 0.1 copy.18
  57.1 0.1 select_reduce_fusion
  57.3 27.1 %all-to-all-done.1 = bf16[128,2,3584]{2,1,0:T(2,128)(2,1)S(1)} async-done(((bf16[128,2,3584]{2,1,0:T(2,128)(2,1)}), bf16[128,2,3584]{2,1,0:T(2,128)(2,1)S(1)}, u32[]{:S(2)}, u32[]{:S(2)}) %all-to-all-start.1) | async-done | bytes 1835040 | tf_op jit(solution)/shard_map/all_to_all | solution.py:114
  84.4 0.2 copy.21
  84.6 0.3 fusion.4
  84.9 1.0 %fusion = bf16[16,3584]{1,0:T(8,128)(2,1)} fusion(f32[16,3584]{1,0:T(8,128)S(1)} %fusion.4, bf16[256,3584]{1,0:T(8,128)(2,1)S(1)} %bitcast.12, f32[16,256]{1,0:T(8,128)S(1)} %select_reduce_fusion), kind=kOutput, calls=%fused_computation.1 | convolution fusion | flops 29487104 | bytes 2195456 | tf_op jit(solution)/shard_map/dot_general | solution.py:122
  (5 shorter events, 0.1 us)
Async XLA Ops:
  1.6 0.9 %copy-start.1 = (bf16[16,3584]{1,0:T(8,128)(2,1)S(1)}, bf16[16,3584]{1,0:T(8,128)(2,1)}, u32[]{:S(2)}) copy-start(bf16[16,3584]{1,0:T(8,128)(2,1)} %tok_ref.1) | copy-start | bytes 344068
  3.4 38.7 %copy-start = (bf16[1,3584,1024]{2,1,0:T(8,128)(2,1)S(1)}, bf16[1,3584,1024]{2,1,0:T(8,128)(2,1)}, u32[]{:S(2)}) copy-start(bf16[1,3584,1024]{2,1,0:T(8,128)(2,1)} %wg_ref.1) | copy-start | bytes 22020100
  52.2 4.8 %copy-start.2 = (s32[16,8]{0,1:T(8,128)S(1)}, s32[16,8]{0,1:T(8,128)}, u32[]{:S(2)}) copy-start(s32[16,8]{0,1:T(8,128)} %param.8) | copy-start | bytes 1540
  52.2 32.2 %all-to-all-start.1 = ((bf16[128,2,3584]{2,1,0:T(2,128)(2,1)}), bf16[128,2,3584]{2,1,0:T(2,128)(2,1)S(1)}, u32[]{:S(2)}, u32[]{:S(2)}) async-start(bf16[128,2,3584]{2,1,0:T(2,128)(2,1)} %shard_map.65), calls=%async_computation.1 | async-start | bytes 3670016 | tf_op jit(solution)/shard_map/all_to_all | solution.py:114

commit v8 on v7

--- a/solution.py
+++ b/solution.py
@@ -117,9 +117,9 @@
     combine = jnp.sum(jnp.where(route_hit, weight[:, :, None], 0.0), axis=1)
     combine_hi = lax.reduce_precision(combine, exponent_bits=8, mantissa_bits=7)
     combine_lo = combine - combine_hi
-    mixed = jnp.dot(
-        combine_hi.astype(jnp.bfloat16), back_flat, preferred_element_type=jnp.float32
-    ) + jnp.dot(combine_lo.astype(jnp.bfloat16), back_flat, preferred_element_type=jnp.float32)
+    split = jnp.concatenate([combine_hi, combine_lo], axis=0).astype(jnp.bfloat16)
+    both = jnp.dot(split, back_flat, preferred_element_type=jnp.float32)
+    mixed = both[:tok_rows] + both[tok_rows:]
     return mixed.astype(jnp.bfloat16)
 
 

time: 86.2 us -> 85.9 us (level)
  matrix products: 1.36 us -> 0.42 us
    dot_general x2 -> x1, matrix products: 1.36 us -> 0.42 us  [local(): both = jnp.dot(split, back_flat, preferred_element_type=jnp.float32)]
where the time goes in v8:
time: 85.9 us; the launch traced here: 85.7 us
  blocking collectives  38.5 us (45%)
  waiting for transfers between devices  27.1 us (32%)
  Pallas kernels  11 us (13%)
  starting transfers between devices  4.81 us (6%)
  local copies, waits for them, and re-layouts  2.22 us (3%)
  other arithmetic  1.5 us (2%)
    all_to_all x1, blocking collectives, local(): lax.all_to_all(outgoing, ('group', 'local'), split_axis=0, concat_axis=0,...  38.5 us
    all_to_all x1, waiting for transfers between devices, local(): lax.all_to_all(produced, ('group', 'local'), split_axis=0, concat_axis=0,...  27.1 us
    pallas_call x1, Pallas kernels, expert_rows(): pl.pallas_call(mlp_kernel, in_specs=[vmem, vmem, anyspace, anyspace], out...  10.1 us
    all_to_all x1, starting transfers between devices, local(): lax.all_to_all(produced, ('group', 'local'), split_axis=0, concat_axis=0,...  4.81 us
    unnamed x8, local copies, waits for them, and re-layouts  1.74 us
  transfers between devices with their start and end apart: 1, of which 1 were waited for; matrix products, arithmetic and copies ran while one was open for 0% of the time, Pallas kernels for 0%

profile of v8, /device:TPU:1, one launch (start us, length us, event | category | flops | bytes accessed | tf_op | source)
XLA Modules:
  0.0 85.7 jit_solution(1877780082775660835)
XLA Ops:
  0.0 0.8 copy.16
  0.8 0.1 convert_reduce_fusion
  0.9 0.4 select_reduce_fusion.1
  1.3 0.1 fusion.1
  1.5 0.1 copy.19
  1.6 0.0 copy-start.1
  1.6 0.9 %copy-done.1 = bf16[16,3584]{1,0:T(8,128)(2,1)S(1)} copy-done((bf16[16,3584]{1,0:T(8,128)(2,1)S(1)}, bf16[16,3584]{1,0:T(8,128)(2,1)}, u32[]{:S(2)}) %copy-start.1) | copy-done | bytes 114712
  2.5 0.9 %shard_map.64 = bf16[128,2,3584]{2,1,0:T(2,128)(2,1)S(1)} custom-call(bf16[2,128,16]{2,1,0:T(8,128)(2,1)S(1)} %bitcast.9, bf16[16,3584]{1,0:T(8,128)(2,1)S(1)} %copy-done.1), custom_call_target="tpu_custom_call" | custom-call | tf_op jit(solution)/shard_map/pallas_call | solution.py:83
  3.4 0.0 copy-start
  3.4 38.5 %all_to_all.10 = bf16[128,2,3584]{2,1,0:T(2,128)(2,1)S(1)} all-to-all(bf16[128,2,3584]{2,1,0:T(2,128)(2,1)S(1)} %shard_map.64), channel_id=1, replica_groups=mesh['group'=16,'local'=8] {'group','local'}, dimensions={0} | all-to-all | bytes 3670016 | tf_op jit(solution)/shard_map/all_to_all | solution.py:111
  41.9 0.2 copy.20
  42.1 0.0 copy-done
  42.1 10.1 %shard_map.65 = bf16[128,2,3584]{2,1,0:T(2,128)(2,1)} custom-call(bf16[256,3584]{1,0:T(8,128)(2,1)S(1)} %bitcast.8, bf16[1,3584,1024]{2,1,0:T(8,128)(2,1)S(1)} %copy-done, bf16[1,3584,1024]{2,1,0:T(8,128)(2,1)} %wu_hbm.1, bf16[1,1024,3584]{2,1,0:T(8,128)(2,1)} %wd_hbm.1), custom_call_target="tpu_custom_call" | custom-call | flops 5637144576 | bytes 25690112 | tf_op jit(solution)/shard_map/pallas_call | solution.py:56
  52.2 0.0 copy-start.2
  52.2 4.8 %all-to-all-start.1 = ((bf16[128,2,3584]{2,1,0:T(2,128)(2,1)}), bf16[128,2,3584]{2,1,0:T(2,128)(2,1)S(1)}, u32[]{:S(2)}, u32[]{:S(2)}) async-start(bf16[128,2,3584]{2,1,0:T(2,128)(2,1)} %shard_map.65), calls=%async_computation.1 | async-start | bytes 3670016 | tf_op jit(solution)/shard_map/all_to_all | solution.py:114
  57.1 0.0 copy-done.2
  57.1 0.1 copy.18
  57.1 0.1 select_reduce_fusion
  57.3 27.1 %all-to-all-done.1 = bf16[128,2,3584]{2,1,0:T(2,128)(2,1)S(1)} async-done(((bf16[128,2,3584]{2,1,0:T(2,128)(2,1)}), bf16[128,2,3584]{2,1,0:T(2,128)(2,1)S(1)}, u32[]{:S(2)}, u32[]{:S(2)}) %all-to-all-start.1) | async-done | bytes 1835040 | tf_op jit(solution)/shard_map/all_to_all | solution.py:114
  84.4 0.2 copy.21
  84.6 0.4 fusion.3
  85.0 0.7 fusion
  (6 shorter events, 0.1 us)
Async XLA Ops:
  1.6 0.9 %copy-start.1 = (bf16[16,3584]{1,0:T(8,128)(2,1)S(1)}, bf16[16,3584]{1,0:T(8,128)(2,1)}, u32[]{:S(2)}) copy-start(bf16[16,3584]{1,0:T(8,128)(2,1)} %tok_ref.1) | copy-start | bytes 344068
  3.4 38.7 %copy-start = (bf16[1,3584,1024]{2,1,0:T(8,128)(2,1)S(1)}, bf16[1,3584,1024]{2,1,0:T(8,128)(2,1)}, u32[]{:S(2)}) copy-start(bf16[1,3584,1024]{2,1,0:T(8,128)(2,1)} %wg_ref.1) | copy-start | bytes 22020100
  52.2 4.8 %copy-start.2 = (s32[16,8]{0,1:T(8,128)S(1)}, s32[16,8]{0,1:T(8,128)}, u32[]{:S(2)}) copy-start(s32[16,8]{0,1:T(8,128)} %param.8) | copy-start | bytes 1540
  52.2 32.2 %all-to-all-start.1 = ((bf16[128,2,3584]{2,1,0:T(2,128)(2,1)}), bf16[128,2,3584]{2,1,0:T(2,128)(2,1)S(1)}, u32[]{:S(2)}, u32[]{:S(2)}) async-start(bf16[128,2,3584]{2,1,0:T(2,128)(2,1)} %shard_map.65), calls=%async_computation.1 | async-start | bytes 3670016 | tf_op jit(solution)/shard_map/all_to_all | solution.py:114

commit v9 on v8

--- a/solution.py
+++ b/solution.py
@@ -69,24 +69,39 @@
     )(rows, w_gate, w_up, w_down)
 
 
-def build_kernel(pick_ref, tok_ref, o_ref):
-    tokens = tok_ref[...]
-    for r in range(o_ref.shape[1]):
-        o_ref[:, r, :] = jnp.dot(
-            pick_ref[r], tokens, preferred_element_type=jnp.float32
-        ).astype(o_ref.dtype)
+def build_kernel(ids_ref, tok_hbm, o_ref, tok_buf, sem):
+    copy = pltpu.make_async_copy(tok_hbm, tok_buf, sem)
+    copy.start()
+    top, tok_rows = ids_ref.shape
+    experts, ranks, _ = o_ref.shape
+    ids = ids_ref[...]
+    expert_col = lax.broadcasted_iota(jnp.int32, (experts, tok_rows), 0)
+    present = ids[0:1, :] == expert_col
+    for k in range(1, top):
+        present = present | (ids[k:k + 1, :] == expert_col)
+    earlier = lax.broadcasted_iota(jnp.int32, (tok_rows, tok_rows), 0) < lax.broadcasted_iota(
+        jnp.int32, (tok_rows, tok_rows), 1
+    )
+    before = jnp.dot(
+        present.astype(jnp.float32), earlier.astype(jnp.float32), preferred_element_type=jnp.float32
+    )
+    copy.wait()
+    tokens = tok_buf[...]
+    for r in range(ranks):
+        pick = jnp.where(present & (before == r), 1.0, 0.0).astype(tokens.dtype)
+        o_ref[:, r, :] = jnp.dot(pick, tokens, preferred_element_type=jnp.float32).astype(o_ref.dtype)
 
 
-def build_rows(pick, tokens):
-    ranks, experts, _ = pick.shape
+def build_rows(ids_t, tokens, experts, ranks):
     vmem = pl.BlockSpec(memory_space=pltpu.VMEM)
     return pl.pallas_call(
         build_kernel,
-        in_specs=[vmem, vmem],
+        in_specs=[vmem, pl.BlockSpec(memory_space=pl.ANY)],
         out_specs=vmem,
         out_shape=jax.ShapeDtypeStruct((experts, ranks, tokens.shape[1]), tokens.dtype),
+        scratch_shapes=[pltpu.VMEM(tokens.shape, tokens.dtype), pltpu.SemaphoreType.DMA(())],
         compiler_params=pltpu.CompilerParams(vmem_limit_bytes=2 * 1024 * 1024),
-    )(pick, tokens)
+    )(ids_t, tokens)
 
 
 def local(tokens, expert_ids, gate_codes, w_gate, w_up, w_down):
@@ -97,6 +112,10 @@
     experts = num_groups * num_local
     capacity = 2 * tok_rows * top // experts
     total_slots = experts * capacity
+    outgoing = build_rows(expert_ids.T, tokens, experts, capacity)
+    got_rows = lax.all_to_all(outgoing, ("group", "local"), split_axis=0, concat_axis=0, tiled=True)
+    expert_ids, got_rows = lax.optimization_barrier((expert_ids, got_rows))
+    rows_in = jnp.swapaxes(got_rows, 0, 1).reshape(total_slots, width)
     expert_range = jnp.arange(experts, dtype=jnp.int32)
     onehot = (expert_ids[:, :, None] == expert_range[None, None, :]).astype(jnp.int32)
     present = jnp.sum(onehot, axis=1)
@@ -106,10 +125,6 @@
     slot_index = jnp.where(kept, slot_rank * experts + expert_ids, total_slots)
     slot_range = jnp.arange(total_slots, dtype=jnp.int32)
     route_hit = slot_index[:, :, None] == slot_range[None, None, :]
-    pick = jnp.any(route_hit, axis=1)
-    outgoing = build_rows(pick.T.astype(jnp.bfloat16).reshape(capacity, experts, tok_rows), tokens)
-    got_rows = lax.all_to_all(outgoing, ("group", "local"), split_axis=0, concat_axis=0, tiled=True)
-    rows_in = jnp.swapaxes(got_rows, 0, 1).reshape(total_slots, width)
     produced = expert_rows(rows_in, w_gate, w_up, w_down)
     returned = lax.all_to_all(produced, ("group", "local"), split_axis=0, concat_axis=0, tiled=True)
     back_flat = jnp.swapaxes(returned, 0, 1).reshape(total_slots, width)

time: 85.9 us -> 85.4 us (level)
    unnamed x8 -> x11, local copies, waits for them, and re-layouts: 1.74 us -> 1.68 us
  transfers between devices with their start and end apart: 1 -> 1, of which waited for: 1 -> 1; matrix products, arithmetic and copies ran while one was open for 0% -> 1% of each run, Pallas kernels for 0% -> 0%
where the time goes in v9:
time: 85.4 us; the launch traced here: 85.2 us
  blocking collectives  38.5 us (45%)
  waiting for transfers between devices  26.5 us (31%)
  Pallas kernels  11.4 us (13%)
  starting transfers between devices  4.82 us (6%)
  local copies, waits for them, and re-layouts  2.11 us (2%)
  other arithmetic  1.37 us (2%)
    all_to_all x1, blocking collectives, local(): lax.all_to_all(outgoing, ('group', 'local'), split_axis=0, concat_axis=0,...  38.5 us
    all_to_all x1, waiting for transfers between devices, local(): lax.all_to_all(produced, ('group', 'local'), split_axis=0, concat_axis=0,...  26.5 us
    pallas_call x1, Pallas kernels, expert_rows(): pl.pallas_call(mlp_kernel, in_specs=[vmem, vmem, anyspace, anyspace], out...  10.1 us
    all_to_all x1, starting transfers between devices, local(): lax.all_to_all(produced, ('group', 'local'), split_axis=0, concat_axis=0,...  4.82 us
  transfers between devices with their start and end apart: 1, of which 1 were waited for; matrix products, arithmetic and copies ran while one was open for 1% of the time, Pallas kernels for 0%

profile of v9, /device:TPU:1, one launch (start us, length us, event | category | flops | bytes accessed | tf_op | source)
XLA Modules:
  0.0 85.2 jit_solution(6044735952590822755)
XLA Ops:
  0.0 0.0 copy-start.1
  0.0 0.9 %copy-done.1 = bf16[16,3584]{1,0:T(8,128)(2,1)S(1)} copy-done((bf16[16,3584]{1,0:T(8,128)(2,1)S(1)}, bf16[16,3584]{1,0:T(8,128)(2,1)}, u32[]{:S(2)}) %copy-start.1) | copy-done | bytes 114712
  0.9 0.0 copy-start.2
  0.9 0.7 copy-done.2
  1.6 1.2 %shard_map.64 = bf16[128,2,3584]{2,1,0:T(2,128)(2,1)S(1)} custom-call(s32[8,16]{1,0:T(8,128)S(1)} %bitcast.7, bf16[16,3584]{1,0:T(8,128)(2,1)S(1)} %copy-done.1), custom_call_target="tpu_custom_call" | custom-call | tf_op jit(solution)/shard_map/pallas_call | solution.py:97
  2.8 0.0 copy-start
  2.9 38.5 %all_to_all.10 = bf16[128,2,3584]{2,1,0:T(2,128)(2,1)S(1)} all-to-all(bf16[128,2,3584]{2,1,0:T(2,128)(2,1)S(1)} %shard_map.64), channel_id=1, replica_groups=mesh['group'=16,'local'=8] {'group','local'}, dimensions={0} | all-to-all | bytes 3670016 | tf_op jit(solution)/shard_map/all_to_all | solution.py:116
  41.4 0.2 copy.19
  41.6 0.0 copy-done
  41.6 10.1 %shard_map.65 = bf16[128,2,3584]{2,1,0:T(2,128)(2,1)} custom-call(bf16[256,3584]{1,0:T(8,128)(2,1)S(1)} %bitcast.6, bf16[1,3584,1024]{2,1,0:T(8,128)(2,1)S(1)} %copy-done, bf16[1,3584,1024]{2,1,0:T(8,128)(2,1)} %wu_hbm.1, bf16[1,1024,3584]{2,1,0:T(8,128)(2,1)} %wd_hbm.1), custom_call_target="tpu_custom_call" | custom-call | flops 5637144576 | bytes 25690112 | tf_op jit(solution)/shard_map/pallas_call | solution.py:56
  51.7 0.0 copy-start.4
  51.7 0.0 copy-start.3
  51.7 4.8 %all-to-all-start.1 = ((bf16[128,2,3584]{2,1,0:T(2,128)(2,1)}), bf16[128,2,3584]{2,1,0:T(2,128)(2,1)S(1)}, u32[]{:S(2)}, u32[]{:S(2)}) async-start(bf16[128,2,3584]{2,1,0:T(2,128)(2,1)} %shard_map.65), calls=%async_computation.1 | async-start | bytes 3670016 | tf_op jit(solution)/shard_map/all_to_all | solution.py:129
  56.5 0.0 copy-done.4
  56.6 0.1 copy.18
  56.6 0.0 copy-done.3
  56.6 0.1 copy.16
  56.7 0.1 convert_reduce_fusion
  56.8 0.4 select_reduce_fusion.1
  57.3 0.1 select_reduce_fusion
  57.4 26.5 %all-to-all-done.1 = bf16[128,2,3584]{2,1,0:T(2,128)(2,1)S(1)} async-done(((bf16[128,2,3584]{2,1,0:T(2,128)(2,1)}), bf16[128,2,3584]{2,1,0:T(2,128)(2,1)S(1)}, u32[]{:S(2)}, u32[]{:S(2)}) %all-to-all-start.1) | async-done | bytes 1835040 | tf_op jit(solution)/shard_map/all_to_all | solution.py:129
  83.9 0.2 copy.20
  84.1 0.4 fusion.2
  84.5 0.7 fusion
  (5 shorter events, 0.1 us)
Async XLA Ops:
  0.0 0.9 %copy-start.1 = (bf16[16,3584]{1,0:T(8,128)(2,1)S(1)}, bf16[16,3584]{1,0:T(8,128)(2,1)}, u32[]{:S(2)}) copy-start(bf16[16,3584]{1,0:T(8,128)(2,1)} %tok_hbm.1) | copy-start | bytes 344068
  0.9 0.7 copy-start.2
  2.8 38.7 %copy-start = (bf16[1,3584,1024]{2,1,0:T(8,128)(2,1)S(1)}, bf16[1,3584,1024]{2,1,0:T(8,128)(2,1)}, u32[]{:S(2)}) copy-start(bf16[1,3584,1024]{2,1,0:T(8,128)(2,1)} %wg_ref.1) | copy-start | bytes 22020100
  51.7 4.9 %copy-start.4 = (s32[16,8]{0,1:T(8,128)S(1)}, s32[16,8]{0,1:T(8,128)}, u32[]{:S(2)}) copy-start(s32[16,8]{0,1:T(8,128)} %param.8) | copy-start | bytes 1540
  51.7 4.9 %copy-start.3 = (s32[16,8]{0,1:T(8,128)S(1)}, s32[16,8]{0,1:T(8,128)}, u32[]{:S(2)}) copy-start(s32[16,8]{0,1:T(8,128)} %param.7) | copy-start | bytes 1540
  51.7 32.2 %all-to-all-start.1 = ((bf16[128,2,3584]{2,1,0:T(2,128)(2,1)}), bf16[128,2,3584]{2,1,0:T(2,128)(2,1)S(1)}, u32[]{:S(2)}, u32[]{:S(2)}) async-start(bf16[128,2,3584]{2,1,0:T(2,128)(2,1)} %shard_map.65), calls=%async_computation.1 | async-start | bytes 3670016 | tf_op jit(solution)/shard_map/all_to_all | solution.py:129

commit v10 on v9

--- a/solution.py
+++ b/solution.py
@@ -69,12 +69,15 @@
     )(rows, w_gate, w_up, w_down)
 
 
-def build_kernel(ids_ref, tok_hbm, o_ref, tok_buf, sem):
-    copy = pltpu.make_async_copy(tok_hbm, tok_buf, sem)
+def build_kernel(ids_hbm, tok_hbm, o_ref, ids_buf, tok_buf, sems):
+    copy = pltpu.make_async_copy(tok_hbm, tok_buf, sems.at[0])
     copy.start()
-    top, tok_rows = ids_ref.shape
+    ids_copy = pltpu.make_async_copy(ids_hbm, ids_buf, sems.at[1])
+    ids_copy.start()
+    top, tok_rows = ids_buf.shape
     experts, ranks, _ = o_ref.shape
-    ids = ids_ref[...]
+    ids_copy.wait()
+    ids = ids_buf[...]
     expert_col = lax.broadcasted_iota(jnp.int32, (experts, tok_rows), 0)
     present = ids[0:1, :] == expert_col
     for k in range(1, top):
@@ -96,11 +99,15 @@
     vmem = pl.BlockSpec(memory_space=pltpu.VMEM)
     return pl.pallas_call(
         build_kernel,
-        in_specs=[vmem, pl.BlockSpec(memory_space=pl.ANY)],
+        in_specs=[pl.BlockSpec(memory_space=pl.ANY), pl.BlockSpec(memory_space=pl.ANY)],
         out_specs=vmem,
         out_shape=jax.ShapeDtypeStruct((experts, ranks, tokens.shape[1]), tokens.dtype),
-        scratch_shapes=[pltpu.VMEM(tokens.shape, tokens.dtype), pltpu.SemaphoreType.DMA(())],
-        compiler_params=pltpu.CompilerParams(vmem_limit_bytes=2 * 1024 * 1024),
+        scratch_shapes=[
+            pltpu.VMEM(ids_t.shape, ids_t.dtype),
+            pltpu.VMEM(tokens.shape, tokens.dtype),
+            pltpu.SemaphoreType.DMA((2,)),
+        ],
+        compiler_params=pltpu.CompilerParams(vmem_limit_bytes=56 * 1024 * 1024),
     )(ids_t, tokens)
 
 

time: 85.4 us -> 86 us (level)
  Pallas kernels: 11.4 us -> 13.2 us
  local copies, waits for them, and re-layouts: 2.11 us -> 0.52 us
    pallas_call x1, Pallas kernels: 1.24 us -> 3.11 us  [build_rows(): pl.pallas_call(build_kernel, in_specs=[pl.BlockSpec(memory_space=pl.ANY),...]
    unnamed x11 -> x7, local copies, waits for them, and re-layouts: 1.68 us -> 0.09 us
where the time goes in v10:
time: 86 us; the launch traced here: 85.7 us
  blocking collectives  38.7 us (45%)
  waiting for transfers between devices  26.5 us (31%)
  Pallas kernels  13.2 us (15%)
  starting transfers between devices  4.83 us (6%)
  other arithmetic  1.37 us (2%)
    all_to_all x1, blocking collectives, local(): lax.all_to_all(outgoing, ('group', 'local'), split_axis=0, concat_axis=0,...  38.7 us
    all_to_all x1, waiting for transfers between devices, local(): lax.all_to_all(produced, ('group', 'local'), split_axis=0, concat_axis=0,...  26.5 us
    pallas_call x1, Pallas kernels, expert_rows(): pl.pallas_call(mlp_kernel, in_specs=[vmem, vmem, anyspace, anyspace], out...  10.1 us
    all_to_all x1, starting transfers between devices, local(): lax.all_to_all(produced, ('group', 'local'), split_axis=0, concat_axis=0,...  4.83 us
    pallas_call x1, Pallas kernels, build_rows(): pl.pallas_call(build_kernel, in_specs=[pl.BlockSpec(memory_space=pl.ANY),...  3.11 us
  transfers between devices with their start and end apart: 1, of which 1 were waited for; matrix products, arithmetic and copies ran while one was open for 1% of the time, Pallas kernels for 0%

profile of v10, /device:TPU:1, one launch (start us, length us, event | category | flops | bytes accessed | tf_op | source)
XLA Modules:
  0.0 85.7 jit_solution(15263321265231803820)
XLA Ops:
  0.0 3.1 %shard_map.64 = bf16[128,2,3584]{2,1,0:T(2,128)(2,1)} custom-call(s32[8,16]{1,0:T(8,128)} %bitcast.10, bf16[16,3584]{1,0:T(8,128)(2,1)} %tok_hbm.1), custom_call_target="tpu_custom_call" | custom-call | tf_op jit(solution)/shard_map/pallas_call | solution.py:100
  3.1 0.0 copy-start
  3.1 38.7 %all_to_all.10 = bf16[128,2,3584]{2,1,0:T(2,128)(2,1)S(1)} all-to-all(bf16[128,2,3584]{2,1,0:T(2,128)(2,1)} %shard_map.64), channel_id=1, replica_groups=mesh['group'=16,'local'=8] {'group','local'}, dimensions={0} | all-to-all | bytes 3670016 | tf_op jit(solution)/shard_map/all_to_all | solution.py:123
  41.9 0.2 copy.19
  42.0 0.0 copy-done
  42.1 10.1 %shard_map.65 = bf16[128,2,3584]{2,1,0:T(2,128)(2,1)} custom-call(bf16[256,3584]{1,0:T(8,128)(2,1)S(1)} %bitcast.6, bf16[1,3584,1024]{2,1,0:T(8,128)(2,1)S(1)} %copy-done, bf16[1,3584,1024]{2,1,0:T(8,128)(2,1)} %wu_hbm.1, bf16[1,1024,3584]{2,1,0:T(8,128)(2,1)} %wd_hbm.1), custom_call_target="tpu_custom_call" | custom-call | flops 5637144576 | bytes 25690112 | tf_op jit(solution)/shard_map/pallas_call | solution.py:56
  52.2 0.0 copy-start.2
  52.2 0.0 copy-start.1
  52.2 4.8 %all-to-all-start.1 = ((bf16[128,2,3584]{2,1,0:T(2,128)(2,1)}), bf16[128,2,3584]{2,1,0:T(2,128)(2,1)S(1)}, u32[]{:S(2)}, u32[]{:S(2)}) async-start(bf16[128,2,3584]{2,1,0:T(2,128)(2,1)} %shard_map.65), calls=%async_computation.1 | async-start | bytes 3670016 | tf_op jit(solution)/shard_map/all_to_all | solution.py:136
  57.0 0.0 copy-done.2
  57.0 0.1 copy.18
  57.1 0.0 copy-done.1
  57.1 0.1 copy.16
  57.2 0.1 convert_reduce_fusion
  57.3 0.4 select_reduce_fusion.1
  57.8 0.1 select_reduce_fusion
  57.9 26.5 %all-to-all-done.1 = bf16[128,2,3584]{2,1,0:T(2,128)(2,1)S(1)} async-done(((bf16[128,2,3584]{2,1,0:T(2,128)(2,1)}), bf16[128,2,3584]{2,1,0:T(2,128)(2,1)S(1)}, u32[]{:S(2)}, u32[]{:S(2)}) %all-to-all-start.1) | async-done | bytes 1835040 | tf_op jit(solution)/shard_map/all_to_all | solution.py:136
  84.4 0.2 copy.20
  84.6 0.4 fusion.2
  85.0 0.7 fusion
  (5 shorter events, 0.1 us)
Async XLA Ops:
  3.1 38.9 %copy-start = (bf16[1,3584,1024]{2,1,0:T(8,128)(2,1)S(1)}, bf16[1,3584,1024]{2,1,0:T(8,128)(2,1)}, u32[]{:S(2)}) copy-start(bf16[1,3584,1024]{2,1,0:T(8,128)(2,1)} %wg_ref.1) | copy-start | bytes 22020100
  52.2 4.9 %copy-start.2 = (s32[16,8]{0,1:T(8,128)S(1)}, s32[16,8]{0,1:T(8,128)}, u32[]{:S(2)}) copy-start(s32[16,8]{0,1:T(8,128)} %param.8) | copy-start | bytes 1540
  52.2 4.9 %copy-start.1 = (s32[16,8]{0,1:T(8,128)S(1)}, s32[16,8]{0,1:T(8,128)}, u32[]{:S(2)}) copy-start(s32[16,8]{0,1:T(8,128)} %param.7) | copy-start | bytes 1540
  52.2 32.2 %all-to-all-start.1 = ((bf16[128,2,3584]{2,1,0:T(2,128)(2,1)}), bf16[128,2,3584]{2,1,0:T(2,128)(2,1)S(1)}, u32[]{:S(2)}, u32[]{:S(2)}) async-start(bf16[128,2,3584]{2,1,0:T(2,128)(2,1)} %shard_map.65), calls=%async_computation.1 | async-start | bytes 3670016 | tf_op jit(solution)/shard_map/all_to_all | solution.py:136

commit v11 on v9

--- a/solution.py
+++ b/solution.py
@@ -104,6 +104,30 @@
     )(ids_t, tokens)
 
 
+def combine_kernel(w_ref, ret_ref, o_ref):
+    tok_rows = o_ref.shape[0]
+    experts, ranks, _ = ret_ref.shape
+    w = w_ref[...]
+    both = None
+    for r in range(ranks):
+        part = jnp.dot(
+            w[:, r * experts:(r + 1) * experts], ret_ref[:, r, :], preferred_element_type=jnp.float32
+        )
+        both = part if both is None else both + part
+    o_ref[...] = (both[:tok_rows] + both[tok_rows:]).astype(o_ref.dtype)
+
+
+def combine_rows(split, returned, tok_rows):
+    vmem = pl.BlockSpec(memory_space=pltpu.VMEM)
+    return pl.pallas_call(
+        combine_kernel,
+        in_specs=[vmem, vmem],
+        out_specs=vmem,
+        out_shape=jax.ShapeDtypeStruct((tok_rows, returned.shape[2]), returned.dtype),
+        compiler_params=pltpu.CompilerParams(vmem_limit_bytes=8 * 1024 * 1024),
+    )(split, returned)
+
+
 def local(tokens, expert_ids, gate_codes, w_gate, w_up, w_down):
     tok_rows, width = tokens.shape
     top = expert_ids.shape[1]
@@ -127,15 +151,12 @@
     route_hit = slot_index[:, :, None] == slot_range[None, None, :]
     produced = expert_rows(rows_in, w_gate, w_up, w_down)
     returned = lax.all_to_all(produced, ("group", "local"), split_axis=0, concat_axis=0, tiled=True)
-    back_flat = jnp.swapaxes(returned, 0, 1).reshape(total_slots, width)
     weight = jnp.where(kept, gate_codes.astype(jnp.float32) / 1024.0, jnp.zeros((), jnp.float32))
     combine = jnp.sum(jnp.where(route_hit, weight[:, :, None], 0.0), axis=1)
     combine_hi = lax.reduce_precision(combine, exponent_bits=8, mantissa_bits=7)
     combine_lo = combine - combine_hi
     split = jnp.concatenate([combine_hi, combine_lo], axis=0).astype(jnp.bfloat16)
-    both = jnp.dot(split, back_flat, preferred_element_type=jnp.float32)
-    mixed = both[:tok_rows] + both[tok_rows:]
-    return mixed.astype(jnp.bfloat16)
+    return combine_rows(split, returned, tok_rows)
 
 
 def solution(mesh):

time: 85.4 us -> 88.7 us (1.039)
  Pallas kernels: 11.4 us -> 15.9 us
    pallas_call x0 -> x1, Pallas kernels: none -> 4.52 us  [combine_rows(): pl.pallas_call(combine_kernel, in_specs=[vmem, vmem], out_specs=vmem, out...]
where the time goes in v11:
time: 88.7 us; the launch traced here: 88.4 us
  blocking collectives  38.5 us (43%)
  waiting for transfers between devices  26.5 us (30%)
  Pallas kernels  15.9 us (18%)
  starting transfers between devices  4.83 us (5%)
  local copies, waits for them, and re-layouts  1.93 us (2%)
    all_to_all x1, blocking collectives, local(): lax.all_to_all(outgoing, ('group', 'local'), split_axis=0, concat_axis=0,...  38.5 us
    all_to_all x1, waiting for transfers between devices, local(): lax.all_to_all(produced, ('group', 'local'), split_axis=0, concat_axis=0,...  26.5 us
    pallas_call x1, Pallas kernels, expert_rows(): pl.pallas_call(mlp_kernel, in_specs=[vmem, vmem, anyspace, anyspace], out...  10.1 us
    all_to_all x1, starting transfers between devices, local(): lax.all_to_all(produced, ('group', 'local'), split_axis=0, concat_axis=0,...  4.83 us
    pallas_call x1, Pallas kernels, combine_rows(): pl.pallas_call(combine_kernel, in_specs=[vmem, vmem], out_specs=vmem, out...  4.52 us
  transfers between devices with their start and end apart: 1, of which 1 were waited for; matrix products, arithmetic and copies ran while one was open for 1% of the time, Pallas kernels for 0%

profile of v11, /device:TPU:1, one launch (start us, length us, event | category | flops | bytes accessed | tf_op | source)
XLA Modules:
  0.0 88.4 jit_solution(18269910054968470608)
XLA Ops:
  0.0 0.0 copy-start.1
  0.0 0.9 %copy-done.1 = bf16[16,3584]{1,0:T(8,128)(2,1)S(1)} copy-done((bf16[16,3584]{1,0:T(8,128)(2,1)S(1)}, bf16[16,3584]{1,0:T(8,128)(2,1)}, u32[]{:S(2)}) %copy-start.1) | copy-done | bytes 114712
  0.9 0.0 copy-start.2
  0.9 0.7 copy-done.2
  1.6 1.2 %shard_map.64 = bf16[128,2,3584]{2,1,0:T(2,128)(2,1)S(1)} custom-call(s32[8,16]{1,0:T(8,128)S(1)} %bitcast.4, bf16[16,3584]{1,0:T(8,128)(2,1)S(1)} %copy-done.1), custom_call_target="tpu_custom_call" | custom-call | tf_op jit(solution)/shard_map/pallas_call | solution.py:97
  2.8 0.0 copy-start
  2.8 38.5 %all_to_all.10 = bf16[128,2,3584]{2,1,0:T(2,128)(2,1)S(1)} all-to-all(bf16[128,2,3584]{2,1,0:T(2,128)(2,1)S(1)} %shard_map.64), channel_id=1, replica_groups=mesh['group'=16,'local'=8] {'group','local'}, dimensions={0} | all-to-all | bytes 3670016 | tf_op jit(solution)/shard_map/all_to_all | solution.py:140
  41.4 0.2 copy.14
  41.6 0.0 copy-done
  41.6 10.1 %shard_map.65 = bf16[128,2,3584]{2,1,0:T(2,128)(2,1)} custom-call(bf16[256,3584]{1,0:T(8,128)(2,1)S(1)} %bitcast.3, bf16[1,3584,1024]{2,1,0:T(8,128)(2,1)S(1)} %copy-done, bf16[1,3584,1024]{2,1,0:T(8,128)(2,1)} %wu_hbm.1, bf16[1,1024,3584]{2,1,0:T(8,128)(2,1)} %wd_hbm.1), custom_call_target="tpu_custom_call" | custom-call | flops 5637144576 | bytes 25690112 | tf_op jit(solution)/shard_map/pallas_call | solution.py:56
  51.7 0.0 copy-start.4
  51.7 0.0 copy-start.3
  51.7 4.8 %all-to-all-start.1 = ((bf16[128,2,3584]{2,1,0:T(2,128)(2,1)}), bf16[128,2,3584]{2,1,0:T(2,128)(2,1)S(1)}, u32[]{:S(2)}, u32[]{:S(2)}) async-start(bf16[128,2,3584]{2,1,0:T(2,128)(2,1)} %shard_map.65), calls=%async_computation.1 | async-start | bytes 3670016 | tf_op jit(solution)/shard_map/all_to_all | solution.py:153
  56.5 0.0 copy-done.4
  56.6 0.1 copy.13
  56.6 0.0 copy-done.3
  56.6 0.1 copy.11
  56.7 0.1 convert_reduce_fusion
  56.8 0.4 select_reduce_fusion.1
  57.3 0.1 select_reduce_fusion
  57.4 26.5 %all-to-all-done.1.ret_ref = bf16[128,2,3584]{2,1,0:T(2,128)(2,1)S(1)} async-done(((bf16[128,2,3584]{2,1,0:T(2,128)(2,1)}), bf16[128,2,3584]{2,1,0:T(2,128)(2,1)S(1)}, u32[]{:S(2)}, u32[]{:S(2)}) %all-to-all-start.1) | async-done | bytes 1835040 | tf_op jit(solution)/shard_map/all_to_all | solution.py:153
  83.9 4.5 %shard_map.66 = bf16[16,3584]{1,0:T(8,128)(2,1)} custom-call(bf16[32,256]{1,0:T(8,128)(2,1)S(1)} %pad_maximum_fusion.w_ref, bf16[128,2,3584]{2,1,0:T(2,128)(2,1)S(1)} %all-to-all-done.1.ret_ref), custom_call_target="tpu_custom_call" | custom-call | tf_op jit(solution)/shard_map/pallas_call | solution.py:122
  (6 shorter events, 0.1 us)
Async XLA Ops:
  0.0 0.9 %copy-start.1 = (bf16[16,3584]{1,0:T(8,128)(2,1)S(1)}, bf16[16,3584]{1,0:T(8,128)(2,1)}, u32[]{:S(2)}) copy-start(bf16[16,3584]{1,0:T(8,128)(2,1)} %tok_hbm.1) | copy-start | bytes 344068
  0.9 0.7 copy-start.2
  2.8 38.7 %copy-start = (bf16[1,3584,1024]{2,1,0:T(8,128)(2,1)S(1)}, bf16[1,3584,1024]{2,1,0:T(8,128)(2,1)}, u32[]{:S(2)}) copy-start(bf16[1,3584,1024]{2,1,0:T(8,128)(2,1)} %wg_ref.1) | copy-start | bytes 22020100
  51.7 4.9 %copy-start.4 = (s32[16,8]{0,1:T(8,128)S(1)}, s32[16,8]{0,1:T(8,128)}, u32[]{:S(2)}) copy-start(s32[16,8]{0,1:T(8,128)} %param.8) | copy-start | bytes 1540
  51.7 4.9 %copy-start.3 = (s32[16,8]{0,1:T(8,128)S(1)}, s32[16,8]{0,1:T(8,128)}, u32[]{:S(2)}) copy-start(s32[16,8]{0,1:T(8,128)} %param.7) | copy-start | bytes 1540
  51.7 32.2 %all-to-all-start.1 = ((bf16[128,2,3584]{2,1,0:T(2,128)(2,1)}), bf16[128,2,3584]{2,1,0:T(2,128)(2,1)S(1)}, u32[]{:S(2)}, u32[]{:S(2)}) async-start(bf16[128,2,3584]{2,1,0:T(2,128)(2,1)} %shard_map.65), calls=%async_computation.1 | async-start | bytes 3670016 | tf_op jit(solution)/shard_map/all_to_all | solution.py:153

commit v12 on v9

--- a/solution.py
+++ b/solution.py
@@ -37,10 +37,11 @@
         hid_ref[:, cols] = (gate_part / (1.0 + jnp.exp(-gate_part)) * up_part).astype(jnp.bfloat16)
     for c in downs:
         c.wait()
-    acc = jnp.dot(hid_ref[...], wd_all[...], preferred_element_type=jnp.float32)
-    half = acc.shape[0] // 2
+    half = hid_ref.shape[0] // 2
+    wd = wd_all[...]
     for r in range(2):
-        o_ref[:, r, :] = acc[r * half:(r + 1) * half].astype(o_ref.dtype)
+        acc = jnp.dot(hid_ref[r * half:(r + 1) * half, :], wd, preferred_element_type=jnp.float32)
+        o_ref[:, r, :] = acc.astype(o_ref.dtype)
 
 
 def expert_rows(rows, w_gate, w_up, w_down):

time: 85.4 us -> 85.5 us (level)
  no operation moved by 1% of the time
where the time goes in v12:
time: 85.5 us; the launch traced here: 85.3 us
  blocking collectives  38.5 us (45%)
  waiting for transfers between devices  26.5 us (31%)
  Pallas kernels  11.4 us (13%)
  starting transfers between devices  4.82 us (6%)
  local copies, waits for them, and re-layouts  2.11 us (2%)
  other arithmetic  1.37 us (2%)
    all_to_all x1, blocking collectives, local(): lax.all_to_all(outgoing, ('group', 'local'), split_axis=0, concat_axis=0,...  38.5 us
    all_to_all x1, waiting for transfers between devices, local(): lax.all_to_all(produced, ('group', 'local'), split_axis=0, concat_axis=0,...  26.5 us
    pallas_call x1, Pallas kernels, expert_rows(): pl.pallas_call(mlp_kernel, in_specs=[vmem, vmem, anyspace, anyspace], out...  10.2 us
    all_to_all x1, starting transfers between devices, local(): lax.all_to_all(produced, ('group', 'local'), split_axis=0, concat_axis=0,...  4.82 us
  transfers between devices with their start and end apart: 1, of which 1 were waited for; matrix products, arithmetic and copies ran while one was open for 1% of the time, Pallas kernels for 0%

profile of v12, /device:TPU:1, one launch (start us, length us, event | category | flops | bytes accessed | tf_op | source)
XLA Modules:
  0.0 85.3 jit_solution(9530002545953718476)
XLA Ops:
  0.0 0.0 copy-start.1
  0.0 0.9 %copy-done.1 = bf16[16,3584]{1,0:T(8,128)(2,1)S(1)} copy-done((bf16[16,3584]{1,0:T(8,128)(2,1)S(1)}, bf16[16,3584]{1,0:T(8,128)(2,1)}, u32[]{:S(2)}) %copy-start.1) | copy-done | bytes 114712
  0.9 0.0 copy-start.2
  0.9 0.7 copy-done.2
  1.6 1.2 %shard_map.64 = bf16[128,2,3584]{2,1,0:T(2,128)(2,1)S(1)} custom-call(s32[8,16]{1,0:T(8,128)S(1)} %bitcast.7, bf16[16,3584]{1,0:T(8,128)(2,1)S(1)} %copy-done.1), custom_call_target="tpu_custom_call" | custom-call | tf_op jit(solution)/shard_map/pallas_call | solution.py:98
  2.8 0.0 copy-start
  2.9 38.5 %all_to_all.10 = bf16[128,2,3584]{2,1,0:T(2,128)(2,1)S(1)} all-to-all(bf16[128,2,3584]{2,1,0:T(2,128)(2,1)S(1)} %shard_map.64), channel_id=1, replica_groups=mesh['group'=16,'local'=8] {'group','local'}, dimensions={0} | all-to-all | bytes 3670016 | tf_op jit(solution)/shard_map/all_to_all | solution.py:117
  41.4 0.2 copy.19
  41.6 0.0 copy-done
  41.6 10.2 %shard_map.65 = bf16[128,2,3584]{2,1,0:T(2,128)(2,1)} custom-call(bf16[256,3584]{1,0:T(8,128)(2,1)S(1)} %bitcast.6, bf16[1,3584,1024]{2,1,0:T(8,128)(2,1)S(1)} %copy-done, bf16[1,3584,1024]{2,1,0:T(8,128)(2,1)} %wu_hbm.1, bf16[1,1024,3584]{2,1,0:T(8,128)(2,1)} %wd_hbm.1), custom_call_target="tpu_custom_call" | custom-call | flops 5637144576 | bytes 25690112 | tf_op jit(solution)/shard_map/pallas_call | solution.py:57
  51.8 0.0 copy-start.4
  51.8 0.0 copy-start.3
  51.8 4.8 %all-to-all-start.1 = ((bf16[128,2,3584]{2,1,0:T(2,128)(2,1)}), bf16[128,2,3584]{2,1,0:T(2,128)(2,1)S(1)}, u32[]{:S(2)}, u32[]{:S(2)}) async-start(bf16[128,2,3584]{2,1,0:T(2,128)(2,1)} %shard_map.65), calls=%async_computation.1 | async-start | bytes 3670016 | tf_op jit(solution)/shard_map/all_to_all | solution.py:130
  56.6 0.0 copy-done.4
  56.6 0.1 copy.18
  56.7 0.0 copy-done.3
  56.7 0.1 copy.16
  56.8 0.1 convert_reduce_fusion
  56.9 0.4 select_reduce_fusion.1
  57.4 0.1 select_reduce_fusion
  57.5 26.5 %all-to-all-done.1 = bf16[128,2,3584]{2,1,0:T(2,128)(2,1)S(1)} async-done(((bf16[128,2,3584]{2,1,0:T(2,128)(2,1)}), bf16[128,2,3584]{2,1,0:T(2,128)(2,1)S(1)}, u32[]{:S(2)}, u32[]{:S(2)}) %all-to-all-start.1) | async-done | bytes 1835040 | tf_op jit(solution)/shard_map/all_to_all | solution.py:130
  84.0 0.2 copy.20
  84.2 0.4 fusion.2
  84.6 0.7 fusion
  (5 shorter events, 0.1 us)
Async XLA Ops:
  0.0 0.9 %copy-start.1 = (bf16[16,3584]{1,0:T(8,128)(2,1)S(1)}, bf16[16,3584]{1,0:T(8,128)(2,1)}, u32[]{:S(2)}) copy-start(bf16[16,3584]{1,0:T(8,128)(2,1)} %tok_hbm.1) | copy-start | bytes 344068
  0.9 0.7 copy-start.2
  2.8 38.7 %copy-start = (bf16[1,3584,1024]{2,1,0:T(8,128)(2,1)S(1)}, bf16[1,3584,1024]{2,1,0:T(8,128)(2,1)}, u32[]{:S(2)}) copy-start(bf16[1,3584,1024]{2,1,0:T(8,128)(2,1)} %wg_ref.1) | copy-start | bytes 22020100
  51.8 4.9 %copy-start.4 = (s32[16,8]{0,1:T(8,128)S(1)}, s32[16,8]{0,1:T(8,128)}, u32[]{:S(2)}) copy-start(s32[16,8]{0,1:T(8,128)} %param.8) | copy-start | bytes 1540
  51.8 4.9 %copy-start.3 = (s32[16,8]{0,1:T(8,128)S(1)}, s32[16,8]{0,1:T(8,128)}, u32[]{:S(2)}) copy-start(s32[16,8]{0,1:T(8,128)} %param.7) | copy-start | bytes 1540
  51.8 32.2 %all-to-all-start.1 = ((bf16[128,2,3584]{2,1,0:T(2,128)(2,1)}), bf16[128,2,3584]{2,1,0:T(2,128)(2,1)S(1)}, u32[]{:S(2)}, u32[]{:S(2)}) async-start(bf16[128,2,3584]{2,1,0:T(2,128)(2,1)} %shard_map.65), calls=%async_computation.1 | async-start | bytes 3670016 | tf_op jit(solution)/shard_map/all_to_all | solution.py:130

commit v13 on v9

--- a/solution.py
+++ b/solution.py
@@ -24,13 +24,12 @@
     up_next.start()
     downs = []
     for j in range(steps):
-        up_now = up_next
+        up_next.wait()
         if j + 1 < steps:
             up_next = fetch_up(j + 1)
             up_next.start()
         downs.append(fetch_down(j))
         downs[-1].start()
-        up_now.wait()
         cols = pl.ds(j * H_BLOCK, H_BLOCK)
         gate_part = jnp.dot(x, wg_ref[0, :, cols], preferred_element_type=jnp.float32)
         up_part = jnp.dot(x, wu_buf[j % 2], preferred_element_type=jnp.float32)

time: 85.4 us -> 87.7 us (1.027)
  Pallas kernels: 11.4 us -> 13.6 us
    pallas_call x1, Pallas kernels: 10.1 us -> 12.3 us  [expert_rows(): pl.pallas_call(mlp_kernel, in_specs=[vmem, vmem, anyspace, anyspace], out...]
where the time goes in v13:
time: 87.7 us; the launch traced here: 87.4 us
  blocking collectives  38.5 us (44%)
  waiting for transfers between devices  26.5 us (30%)
  Pallas kernels  13.6 us (16%)
  starting transfers between devices  4.82 us (5%)
  local copies, waits for them, and re-layouts  2.11 us (2%)
  other arithmetic  1.37 us (2%)
    all_to_all x1, blocking collectives, local(): lax.all_to_all(outgoing, ('group', 'local'), split_axis=0, concat_axis=0,...  38.5 us
    all_to_all x1, waiting for transfers between devices, local(): lax.all_to_all(produced, ('group', 'local'), split_axis=0, concat_axis=0,...  26.5 us
    pallas_call x1, Pallas kernels, expert_rows(): pl.pallas_call(mlp_kernel, in_specs=[vmem, vmem, anyspace, anyspace], out...  12.3 us
    all_to_all x1, starting transfers between devices, local(): lax.all_to_all(produced, ('group', 'local'), split_axis=0, concat_axis=0,...  4.82 us
  transfers between devices with their start and end apart: 1, of which 1 were waited for; matrix products, arithmetic and copies ran while one was open for 1% of the time, Pallas kernels for 0%

profile of v13, /device:TPU:1, one launch (start us, length us, event | category | flops | bytes accessed | tf_op | source)
XLA Modules:
  0.0 87.4 jit_solution(2609423188745277226)
XLA Ops:
  0.0 0.0 copy-start.1
  0.0 0.9 %copy-done.1 = bf16[16,3584]{1,0:T(8,128)(2,1)S(1)} copy-done((bf16[16,3584]{1,0:T(8,128)(2,1)S(1)}, bf16[16,3584]{1,0:T(8,128)(2,1)}, u32[]{:S(2)}) %copy-start.1) | copy-done | bytes 114712
  0.9 0.0 copy-start.2
  0.9 0.7 copy-done.2
  1.6 1.2 %shard_map.64 = bf16[128,2,3584]{2,1,0:T(2,128)(2,1)S(1)} custom-call(s32[8,16]{1,0:T(8,128)S(1)} %bitcast.7, bf16[16,3584]{1,0:T(8,128)(2,1)S(1)} %copy-done.1), custom_call_target="tpu_custom_call" | custom-call | tf_op jit(solution)/shard_map/pallas_call | solution.py:96
  2.8 0.0 copy-start
  2.9 38.5 %all_to_all.10 = bf16[128,2,3584]{2,1,0:T(2,128)(2,1)S(1)} all-to-all(bf16[128,2,3584]{2,1,0:T(2,128)(2,1)S(1)} %shard_map.64), channel_id=1, replica_groups=mesh['group'=16,'local'=8] {'group','local'}, dimensions={0} | all-to-all | bytes 3670016 | tf_op jit(solution)/shard_map/all_to_all | solution.py:115
  41.4 0.2 copy.19
  41.6 0.0 copy-done
  41.6 12.3 %shard_map.65 = bf16[128,2,3584]{2,1,0:T(2,128)(2,1)} custom-call(bf16[256,3584]{1,0:T(8,128)(2,1)S(1)} %bitcast.6, bf16[1,3584,1024]{2,1,0:T(8,128)(2,1)S(1)} %copy-done, bf16[1,3584,1024]{2,1,0:T(8,128)(2,1)} %wu_hbm.1, bf16[1,1024,3584]{2,1,0:T(8,128)(2,1)} %wd_hbm.1), custom_call_target="tpu_custom_call" | custom-call | flops 5637144576 | bytes 25690112 | tf_op jit(solution)/shard_map/pallas_call | solution.py:55
  53.9 0.0 copy-start.4
  53.9 0.0 copy-start.3
  53.9 4.8 %all-to-all-start.1 = ((bf16[128,2,3584]{2,1,0:T(2,128)(2,1)}), bf16[128,2,3584]{2,1,0:T(2,128)(2,1)S(1)}, u32[]{:S(2)}, u32[]{:S(2)}) async-start(bf16[128,2,3584]{2,1,0:T(2,128)(2,1)} %shard_map.65), calls=%async_computation.1 | async-start | bytes 3670016 | tf_op jit(solution)/shard_map/all_to_all | solution.py:128
  58.8 0.0 copy-done.4
  58.8 0.1 copy.18
  58.9 0.0 copy-done.3
  58.9 0.1 copy.16
  58.9 0.1 convert_reduce_fusion
  59.1 0.4 select_reduce_fusion.1
  59.5 0.1 select_reduce_fusion
  59.7 26.5 %all-to-all-done.1 = bf16[128,2,3584]{2,1,0:T(2,128)(2,1)S(1)} async-done(((bf16[128,2,3584]{2,1,0:T(2,128)(2,1)}), bf16[128,2,3584]{2,1,0:T(2,128)(2,1)S(1)}, u32[]{:S(2)}, u32[]{:S(2)}) %all-to-all-start.1) | async-done | bytes 1835040 | tf_op jit(solution)/shard_map/all_to_all | solution.py:128
  86.1 0.2 copy.20
  86.3 0.4 fusion.2
  86.7 0.7 fusion
  (5 shorter events, 0.1 us)
Async XLA Ops:
  0.0 0.9 %copy-start.1 = (bf16[16,3584]{1,0:T(8,128)(2,1)S(1)}, bf16[16,3584]{1,0:T(8,128)(2,1)}, u32[]{:S(2)}) copy-start(bf16[16,3584]{1,0:T(8,128)(2,1)} %tok_hbm.1) | copy-start | bytes 344068
  0.9 0.7 copy-start.2
  2.8 38.7 %copy-start = (bf16[1,3584,1024]{2,1,0:T(8,128)(2,1)S(1)}, bf16[1,3584,1024]{2,1,0:T(8,128)(2,1)}, u32[]{:S(2)}) copy-start(bf16[1,3584,1024]{2,1,0:T(8,128)(2,1)} %wg_ref.1) | copy-start | bytes 22020100
  53.9 4.9 %copy-start.4 = (s32[16,8]{0,1:T(8,128)S(1)}, s32[16,8]{0,1:T(8,128)}, u32[]{:S(2)}) copy-start(s32[16,8]{0,1:T(8,128)} %param.8) | copy-start | bytes 1540
  53.9 4.9 %copy-start.3 = (s32[16,8]{0,1:T(8,128)S(1)}, s32[16,8]{0,1:T(8,128)}, u32[]{:S(2)}) copy-start(s32[16,8]{0,1:T(8,128)} %param.7) | copy-start | bytes 1540
  53.9 32.2 %all-to-all-start.1 = ((bf16[128,2,3584]{2,1,0:T(2,128)(2,1)}), bf16[128,2,3584]{2,1,0:T(2,128)(2,1)S(1)}, u32[]{:S(2)}, u32[]{:S(2)}) async-start(bf16[128,2,3584]{2,1,0:T(2,128)(2,1)} %shard_map.65), calls=%async_computation.1 | async-start | bytes 3670016 | tf_op jit(solution)/shard_map/all_to_all | solution.py:128
